TPU v7x, 1024 devices: a whole 4x8x16 slice. The times are simulated.
1024 devices in a mesh: dp: 16 (over y, core), expert: 64 (over z, x).
Axes of the slice: x: 4, y: 8, z: 16, core: 2. Of those that a mesh axis runs over, the one named last changes fastest.
Arguments:
- expert_ids: int32 [131072, 4], P(('dp', 'expert')), may hold values from 0 to 63, all different within a row; in each aligned block of 128 rows (0 to 127, 128 to 255, ...) at most 16 rows name the same one
- route_weight: float32 [131072, 4], P(('dp', 'expert')), may hold values from 0.05 to 0.5
- d_gate: bfloat16 [1048576, 768], P(('dp', 'expert')), may hold values from -6 to 6
- gate_weight: bfloat16 [65536, 768], P('expert'), may hold values from -0.21875 to 0.21875
- projector: bfloat16 [1024, 1280], replicated, may hold values from -0.1875 to 0.1875
- enc_pre: bfloat16 [196608, 1280], P(('dp', 'expert')), may hold values from -6 to 6
- span_lengths: int32 [1024, 8], P(('dp', 'expert')), may hold values from 1 to 12, 64 in all within a row
- span_owner: int32 [1024, 8], P(('dp', 'expert')), may hold values from 0 to 15, as said below
- audio_pos: int32 [1024, 64], P(('dp', 'expert')), may hold values from 0 to 127, as said below
Outputs:
- token_grad: bfloat16 [131072, 1024], P(('dp', 'expert'))
- enc_grad: bfloat16 [196608, 1280], P(('dp', 'expert'))
Inputs may be any that keep to these rules, and one draw needn't show every extreme that they name: `expert_ids`: each row names 4 different experts; among the rows of one device no expert is named more than 16 times, and some device reaches it. `span_lengths`: each row holds one device's 8 span lengths in order, summing to 64, the largest exactly 12. `span_owner`: the owners of one device's spans are all different. `audio_pos`: each row holds 64 different positions, rising.
All inputs are finite; a program needn't handle non-finite values.
Results may differ from a plain program's by a relative error of at most 0.0064.
Values may be sent and summed in bfloat16 or wider, within the bound.
No kernel may reach another device: no remote copies, remote signals or barrier semaphores. Data moves between devices by JAX's collectives and lax.ppermute only.
A program may use at most 32 MiB of HBM per device.

v0:
```python
import jax
import jax.numpy as jnp
from jax import lax
from jax.sharding import PartitionSpec as P

D = 1024


def gelu_slope(values):
    normal_cdf = 0.5 * (1.0 + jax.scipy.special.erf(values * 0.7071067811865476))
    density = jnp.exp(-0.5 * values * values) * 0.3989422804014327
    return normal_cdf + values * density


def body(
    expert_ids,
    route_weight,
    d_gate,
    gate_weight,
    projector,
    enc_pre,
    span_lengths,
    span_owner,
    audio_pos,
):
    groups = lax.axis_size("expert")
    exp_dev = gate_weight.shape[0] // D
    experts_all = exp_dev * groups
    capacity_each = d_gate.shape[0] // experts_all
    slot_count = exp_dev * capacity_each
    hidden_width = gate_weight.shape[1]
    incoming = d_gate.reshape(groups, exp_dev, capacity_each, hidden_width)
    weights = gate_weight.reshape(exp_dev, D, hidden_width)
    outgoing = jnp.einsum("sjrf,jdf->sjrd", incoming, weights, preferred_element_type=jnp.float32)
    outgoing = outgoing.astype(jnp.bfloat16).reshape(groups, slot_count, D)
    returned = lax.all_to_all(outgoing, "expert", split_axis=0, concat_axis=0, tiled=True)
    token_count, top_count = expert_ids.shape
    flat_ids = expert_ids.reshape(-1)
    onehot = (flat_ids[:, None] == jnp.arange(experts_all, dtype=jnp.int32)[None, :]).astype(
        jnp.int32
    )
    route_rank = jnp.sum(jnp.cumsum(onehot, axis=0) * onehot, axis=1) - 1
    target = flat_ids // exp_dev * slot_count + flat_ids % exp_dev * capacity_each + route_rank
    picked = returned.reshape(groups * slot_count, D)[target].reshape(token_count, top_count, D)
    token_grad = jnp.sum(route_weight[:, :, None] * picked.astype(jnp.float32), axis=1).astype(
        jnp.bfloat16
    )
    positions = audio_pos[0]
    lengths = span_lengths[0]
    owners = span_owner[0]
    audio_count = positions.shape[0]
    peer_count = lax.axis_size("dp")
    span_cap = enc_pre.shape[0] // peer_count
    starts = jnp.cumsum(lengths) - lengths
    audio_index = jnp.arange(audio_count, dtype=jnp.int32)
    span_of = jnp.sum((audio_index[:, None] >= starts[None, :]).astype(jnp.int32), axis=1) - 1
    offset = audio_index - starts[span_of]
    place_at = owners[span_of] * span_cap + offset
    audio_rows = token_grad[positions]
    parcel = jnp.zeros((peer_count * span_cap, D), jnp.bfloat16).at[place_at].set(audio_rows)
    arrived_rows = lax.all_to_all(
        parcel.reshape(peer_count, span_cap, D), "dp", split_axis=0, concat_axis=0, tiled=True
    )
    arrived_rows = arrived_rows.reshape(peer_count * span_cap, D)
    arrived = jnp.dot(arrived_rows, projector, preferred_element_type=jnp.float32).astype(
        jnp.bfloat16
    )
    gelu_factor = gelu_slope(enc_pre.astype(jnp.float32))
    enc_grad = (lax.optimization_barrier(arrived).astype(jnp.float32) * gelu_factor).astype(
        jnp.bfloat16
    )
    return (token_grad, enc_grad)


def solution(mesh):
    in_specs = (
        P(("dp", "expert"), None),
        P(("dp", "expert"), None),
        P(("dp", "expert"), None),
        P("expert", None),
        P(),
        P(("dp", "expert"), None),
        P(("dp", "expert"), None),
        P(("dp", "expert"), None),
        P(("dp", "expert"), None),
    )
    out_specs = (P(("dp", "expert"), None), P(("dp", "expert"), None))
    return jax.shard_map(body, mesh=mesh, in_specs=in_specs, out_specs=out_specs, check_vma=False)
```

profile of v0, /device:TPU:1, one launch (start us, length us, event | category | flops | bytes accessed | tf_op | source)
XLA Modules:
  0.0 172.2 jit_solution(426866459454865763)
XLA Ops:
  0.6 0.0 copy-start
  0.6 3.9 %convert_bitcast_fusion = bf16[64,16,1024]{2,0,1:T(8,128)(2,1)S(1)} fusion(bf16[1024,768]{1,0:T(8,128)(2,1)} %param.12, bf16[64,16,768]{2,1,0:T(8,128)(2,1)} %bitcast.128), kind=kOutput, calls=%fused_computation.5 | convolution fusion | flops 1611661312 | bytes 5242880 | tf_op jit(solution)/shard_map/sjrf,jdf->sjrd/dot_general | solution.py:34
  4.5 2.4 %copy.29 = bf16[64,16,1024]{2,1,0:T(8,128)(2,1)} copy(bf16[64,16,1024]{2,0,1:T(8,128)(2,1)S(1)} %convert_bitcast_fusion) | data formatting | bytes 4194304 | tf_op jit(solution)/shard_map/reshape | solution.py:35
  7.0 0.0 copy-start.4
  7.0 0.0 copy-start.5
  7.0 0.0 copy-start.7
  7.0 0.0 copy-start.6
  7.0 0.0 copy-start.3
  7.0 23.2 %all-to-all-start = ((bf16[64,16,1024]{2,1,0:T(8,128)(2,1)}), bf16[64,16,1024]{2,1,0:T(8,128)(2,1)}, u32[]{:S(2)}, u32[]{:S(2)}) async-start(bf16[64,16,1024]{2,1,0:T(8,128)(2,1)} %copy.29), calls=%async_computation | async-start | bytes 4194304 | tf_op jit(solution)/shard_map/all_to_all | solution.py:36
  30.2 0.0 copy-done.4
  30.2 0.1 copy.31
  30.3 0.1 eq.27
  30.4 0.1 eq.31
  30.5 0.1 copy.30
  30.6 0.1 add.121
  30.8 1.2 reduce-window.10
  32.0 0.2 slice_reduce_fusion
  32.2 0.0 copy-done.5
  32.2 0.1 copy.27
  32.4 0.0 copy-done.7
  32.4 0.2 reduce-window.14
  32.6 0.1 fusion.13
  32.7 0.0 copy-done.6
  32.8 0.7 fusion.27
  33.4 0.0 copy-done.3
  33.4 0.7 fusion.26
  34.1 0.1 convert_reduce_fusion
  34.2 9.9 %fusion.23 = s32[64]{0:T(128)S(1)} fusion(s32[64]{0:T(128)S(1)} %convert_reduce_fusion, s32[]{:T(128)} %bitcast.28, s32[]{:T(128)} %bitcast.16, s32[]{:T(128)} %bitcast.29, s32[]{:T(128)} %bitcast.17, s32[]{:T(128)} %bitcast.30, s32[]{:T(128)} %bitcast.18, s32[]{:T(128)} %bitcast.31, s32[]{:T(128)} %bitcast.19, s32[]{:T(128)} %bitcast.32, s32[]{:T(128)} %bitcast.20, ...), kind=kLoop, calls=%fused_computation.62 | loop fusion | flops 1984 | bytes 576 | tf_op jit(solution)/shard_map/select_n | solution.py:60
  44.1 80.9 %all-to-all-done = bf16[64,16,1024]{2,1,0:T(8,128)(2,1)} async-done(((bf16[64,16,1024]{2,1,0:T(8,128)(2,1)}), bf16[64,16,1024]{2,1,0:T(8,128)(2,1)}, u32[]{:S(2)}, u32[]{:S(2)}) %all-to-all-start) | async-done | bytes 2097184 | tf_op jit(solution)/shard_map/all_to_all | solution.py:36
  125.0 5.3 %gather_fusion = bf16[512,1024]{1,0:T(8,128)(2,1)} fusion(bf16[1024,1024]{1,0:T(8,128)(2,1)} %bitcast.5, s32[1024]{0:T(1024)S(1)} %pad_clamp_fusion.1), kind=kCustom, calls=%fused_computation | custom fusion | bytes 2099200 | tf_op jit(solution)/shard_map/gather | solution.py:44
  130.4 2.7 %reshape.182 = f32[128,4,1024]{2,1,0:T(4,128)} reshape(bf16[512,1024]{1,0:T(8,128)(2,1)} %gather_fusion) | data formatting | bytes 3145728 | tf_op jit(solution)/shard_map/convert_element_type | solution.py:45
  133.1 3.0 %multiply_reduce_fusion = bf16[128,1024]{1,0:T(8,128)(2,1)S(1)} fusion(f32[128,4,1024]{2,1,0:T(4,128)} %reshape.182, f32[128,4]{1,0:T(8,128)S(1)} %copy.27), kind=kLoop, calls=%fused_computation.4 | loop fusion | flops 917504 | bytes 2361344 | tf_op jit(solution)/shard_map/reduce_sum | solution.py:45
  136.1 0.0 copy-start.2
  136.1 0.7 copy-done.2
  136.8 1.5 scatter_custom_fusion
  138.3 0.1 reshape.180
  138.4 30.4 %all_to_all.10 = bf16[16,12,1024]{2,1,0:T(8,128)(2,1)} all-to-all(bf16[16,12,1024]{2,1,0:T(8,128)(2,1)S(1)} %reshape.180), channel_id=1, replica_groups=mesh['dp'=16,'expert'=64] {'dp'}, dimensions={0} | all-to-all | bytes 786432 | tf_op jit(solution)/shard_map/all_to_all | solution.py:61
  168.8 1.1 reshape.181
  169.9 0.0 copy-done
  169.9 0.0 copy-start.1
  169.9 0.7 convolution_convert_fusion
  170.6 0.3 copy-done.1
  171.0 1.2 fusion.9
  (11 shorter events, 0.1 us)
Async XLA Ops:
  0.6 169.3 %copy-start = (bf16[1024,1280]{1,0:T(8,128)(2,1)S(1)}, bf16[1024,1280]{1,0:T(8,128)(2,1)}, u32[]{:S(2)}) copy-start(bf16[1024,1280]{1,0:T(8,128)(2,1)} %param.13) | copy-start | bytes 7864324
  7.0 23.2 %copy-start.4 = (s32[128,4]{0,1:T(4,128)S(1)}, s32[128,4]{0,1:T(4,128)}, u32[]{:S(2)}) copy-start(s32[128,4]{0,1:T(4,128)} %param.9) | copy-start | bytes 6148
  7.0 25.3 %copy-start.5 = (f32[128,4]{0,1:T(4,128)S(1)}, f32[128,4]{0,1:T(4,128)}, u32[]{:S(2)}) copy-start(f32[128,4]{0,1:T(4,128)} %param.10) | copy-start | bytes 6148
  7.0 25.4 %copy-start.7 = (s32[1,8]{1,0:T(1,128)S(1)}, s32[1,8]{1,0:T(1,128)}, u32[]{:S(2)}) copy-start(s32[1,8]{1,0:T(1,128)} %param.15) | copy-start | bytes 100
  7.0 25.7 %copy-start.6 = (s32[1,64]{1,0:T(1,128)S(1)}, s32[1,64]{1,0:T(1,128)}, u32[]{:S(2)}) copy-start(s32[1,64]{1,0:T(1,128)} %param.17) | copy-start | bytes 772
  7.0 26.5 %copy-start.3 = (s32[1,8]{1,0:T(1,128)S(1)}, s32[1,8]{1,0:T(1,128)}, u32[]{:S(2)}) copy-start(s32[1,8]{1,0:T(1,128)} %param.16) | copy-start | bytes 100
  7.0 118.0 %all-to-all-start = ((bf16[64,16,1024]{2,1,0:T(8,128)(2,1)}), bf16[64,16,1024]{2,1,0:T(8,128)(2,1)}, u32[]{:S(2)}, u32[]{:S(2)}) async-start(bf16[64,16,1024]{2,1,0:T(8,128)(2,1)} %copy.29), calls=%async_computation | async-start | bytes 4194304 | tf_op jit(solution)/shard_map/all_to_all | solution.py:36
  136.1 0.7 copy-start.2
  169.9 1.0 copy-start.1
where the time goes:
time: 173 us; the launch traced here: 172 us
  waiting for transfers between devices  80.9 us (47%)
  blocking collectives  30.4 us (18%)
  starting transfers between devices  23.2 us (13%)
  local copies, waits for them, and re-layouts  16.5 us (10%)
  other arithmetic  15.9 us (9%)
  matrix products  4.54 us (3%)
    all_to_all x1, waiting for transfers between devices, body(): lax.all_to_all(outgoing, 'expert', split_axis=0, concat_axis=0, tiled=True)  80.9 us
    all_to_all x1, blocking collectives, body(): lax.all_to_all(parcel.reshape(peer_count, span_cap, D), 'dp', split_axis=...  30.4 us
    all_to_all x1, starting transfers between devices, body(): lax.all_to_all(outgoing, 'expert', split_axis=0, concat_axis=0, tiled=True)  23.2 us
    select_n x1, other arithmetic, body(): jnp.zeros((peer_count * span_cap, D), jnp.bfloat16).at[place_at]  9.95 us
    gather x1, local copies, waits for them, and re-layouts, body(): returned.reshape(groups * slot_count, D)[target]  5.35 us
    dot_general x1, matrix products, body(): jnp.einsum('sjrf,jdf->sjrd', incoming, weights, preferred_element_type=jn...  3.86 us
  transfers between devices with their start and end apart: 1, of which 1 were waited for; matrix products, arithmetic and copies ran while one was open for 8% of the time, Pallas kernels for 0%

commit v1 on v0

--- a/solution.py
+++ b/solution.py
@@ -1,9 +1,11 @@
 import jax
 import jax.numpy as jnp
 from jax import lax
+from jax.sharding import Mesh
 from jax.sharding import PartitionSpec as P
 
 D = 1024
+X_PART = 4
 
 
 def gelu_slope(values):
@@ -23,28 +25,47 @@
     span_owner,
     audio_pos,
 ):
-    groups = lax.axis_size("expert")
+    nz = lax.axis_size("ez")
+    nx = lax.axis_size("ex")
+    groups = nz * nx
     exp_dev = gate_weight.shape[0] // D
     experts_all = exp_dev * groups
     capacity_each = d_gate.shape[0] // experts_all
-    slot_count = exp_dev * capacity_each
     hidden_width = gate_weight.shape[1]
+    column_rows = nx * exp_dev * capacity_each
+
     incoming = d_gate.reshape(groups, exp_dev, capacity_each, hidden_width)
     weights = gate_weight.reshape(exp_dev, D, hidden_width)
     outgoing = jnp.einsum("sjrf,jdf->sjrd", incoming, weights, preferred_element_type=jnp.float32)
-    outgoing = outgoing.astype(jnp.bfloat16).reshape(groups, slot_count, D)
-    returned = lax.all_to_all(outgoing, "expert", split_axis=0, concat_axis=0, tiled=True)
+    outgoing = outgoing.astype(jnp.bfloat16).reshape(nz, nx, exp_dev * capacity_each, D)
+    got = lax.all_to_all(outgoing, "ex", split_axis=1, concat_axis=1, tiled=True)
+    got = got.reshape(nz, column_rows, D)
+
     token_count, top_count = expert_ids.shape
     flat_ids = expert_ids.reshape(-1)
     onehot = (flat_ids[:, None] == jnp.arange(experts_all, dtype=jnp.int32)[None, :]).astype(
         jnp.int32
     )
     route_rank = jnp.sum(jnp.cumsum(onehot, axis=0) * onehot, axis=1) - 1
-    target = flat_ids // exp_dev * slot_count + flat_ids % exp_dev * capacity_each + route_rank
-    picked = returned.reshape(groups * slot_count, D)[target].reshape(token_count, top_count, D)
-    token_grad = jnp.sum(route_weight[:, :, None] * picked.astype(jnp.float32), axis=1).astype(
-        jnp.bfloat16
-    )
+    device_of = flat_ids // exp_dev
+    column_of = device_of // nx
+    row_in_column = ((device_of % nx) * exp_dev + flat_ids % exp_dev) * capacity_each + route_rank
+    code = (column_of * column_rows + row_in_column).reshape(token_count, top_count)
+    codes = lax.all_gather(code, "ez")
+    route_weights = lax.all_gather(route_weight, "ez")
+
+    here = lax.axis_index("ez")
+    in_column = codes // column_rows == here
+    share = jnp.where(in_column, route_weights, jnp.zeros_like(route_weights))
+    picks = (codes % column_rows)[..., None] == jnp.arange(column_rows, dtype=jnp.int32)
+    mix = jnp.sum(jnp.where(picks, share[..., None], 0.0), axis=2)
+    mix_hi = mix.astype(jnp.bfloat16)
+    mix_lo = (mix - mix_hi.astype(jnp.float32)).astype(jnp.bfloat16)
+    partial = jnp.einsum("ztr,zrd->ztd", mix_hi, got, preferred_element_type=jnp.float32)
+    partial = partial + jnp.einsum("ztr,zrd->ztd", mix_lo, got, preferred_element_type=jnp.float32)
+    partial = partial.astype(jnp.bfloat16).reshape(nz * token_count, D)
+    token_grad = lax.psum_scatter(partial, "ez", scatter_dimension=0, tiled=True)
+
     positions = audio_pos[0]
     lengths = span_lengths[0]
     owners = span_owner[0]
@@ -73,16 +94,19 @@
 
 
 def solution(mesh):
+    n_dp, n_expert = mesh.devices.shape
+    split = Mesh(mesh.devices.reshape(n_dp, n_expert // X_PART, X_PART), ("dp", "ez", "ex"))
+    rows = P(("dp", "ez", "ex"), None)
     in_specs = (
-        P(("dp", "expert"), None),
-        P(("dp", "expert"), None),
-        P(("dp", "expert"), None),
-        P("expert", None),
+        rows,
+        rows,
+        rows,
+        P(("ez", "ex"), None),
         P(),
-        P(("dp", "expert"), None),
-        P(("dp", "expert"), None),
-        P(("dp", "expert"), None),
-        P(("dp", "expert"), None),
+        rows,
+        rows,
+        rows,
+        rows,
     )
-    out_specs = (P(("dp", "expert"), None), P(("dp", "expert"), None))
-    return jax.shard_map(body, mesh=mesh, in_specs=in_specs, out_specs=out_specs, check_vma=False)
+    out_specs = (rows, rows)
+    return jax.shard_map(body, mesh=split, in_specs=in_specs, out_specs=out_specs, check_vma=False)

time: 173 us -> 238 us (1.38)
  blocking collectives: 30.4 us -> 98.7 us
  starting transfers between devices: 23.2 us -> 4.97 us
  between operations: 0.83 us -> 14.2 us
  waiting for transfers between devices: 80.9 us -> 68 us
  local copies, waits for them, and re-layouts: 16.5 us -> 22.5 us
  matrix products: 4.54 us -> 10.4 us
  other arithmetic: 15.9 us -> 18.8 us
    all_to_all x1, waiting for transfers between devices: 80.9 us -> 0.01 us  [body(): lax.all_to_all(outgoing, 'ex', split_axis=1, concat_axis=1, tiled=True)]
    reduce_scatter x0 -> x1, waiting for transfers between devices: none -> 68 us  [body(): lax.psum_scatter(partial, 'ez', scatter_dimension=0, tiled=True)]
    all_gather x0 -> x2, blocking collectives: none -> 64.6 us  [the longest x1 37.6 us: body(): route_weights = lax.all_gather(route_weight, 'ez')]
    all_to_all x1, starting transfers between devices: 23.2 us -> 4.96 us  [body(): lax.all_to_all(outgoing, 'ex', split_axis=1, concat_axis=1, tiled=True)]
    select_n x1 -> x2, other arithmetic: 0.01 us -> 5.5 us  [the longest x1 2.87 us: body(): share = jnp.where(in_column, route_weights, jnp.zeros_like(route_weights))]
    gather x1 -> x0, local copies, waits for them, and re-layouts: 5.35 us -> none  [body(): returned.reshape(groups * slot_count, D)[target]]
    reshape x1 -> x2, local copies, waits for them, and re-layouts: 2.45 us -> 7.69 us  [body(): outgoing.astype(jnp.bfloat16).reshape(nz, nx, exp_dev * capacity_each, D)]
    dot_general x0 -> x2, matrix products: none -> 4.53 us  [the longest x1 3.24 us: body(): jnp.einsum('ztr,zrd->ztd', mix_lo, got, preferred_element_type=jnp.float32)]
  transfers between devices with their start and end apart: 1 -> 2, of which waited for: 1 -> 1; matrix products, arithmetic and copies ran while one was open for 8% -> 10% of each run, Pallas kernels for 0% -> 0%
where the time goes in v1:
time: 238 us
  blocking collectives  98.7 us (41%)
  waiting for transfers between devices  68 us (29%)
  local copies, waits for them, and re-layouts  22.5 us (9%)
  other arithmetic  18.8 us (8%)
  between operations  14.2 us (6%)
  matrix products  10.4 us (4%)
  starting transfers between devices  4.97 us (2%)
    reduce_scatter x1, waiting for transfers between devices, body(): lax.psum_scatter(partial, 'ez', scatter_dimension=0, tiled=True)  68 us
    all_gather x1, blocking collectives, body(): route_weights = lax.all_gather(route_weight, 'ez')  37.6 us
    all_to_all x1, blocking collectives, body(): lax.all_to_all(parcel.reshape(peer_count, span_cap, D), 'dp', split_axis=...  34.1 us
    all_gather x1, blocking collectives, body(): codes = lax.all_gather(code, 'ez')  26.9 us
    select_n x1, other arithmetic, body(): jnp.zeros((peer_count * span_cap, D), jnp.bfloat16).at[place_at]  9.98 us
    reshape x2, local copies, waits for them, and re-layouts, body(): outgoing.astype(jnp.bfloat16).reshape(nz, nx, exp_dev * capacity_each, D)  7.69 us
    dot_general x1, matrix products, body(): jnp.einsum('sjrf,jdf->sjrd', incoming, weights, preferred_element_type=jn...  5.22 us
    all_to_all x1, starting transfers between devices, body(): lax.all_to_all(outgoing, 'ex', split_axis=1, concat_axis=1, tiled=True)  4.96 us
  transfers between devices with their start and end apart: 2, of which 1 were waited for; matrix products, arithmetic and copies ran while one was open for 10% of the time, Pallas kernels for 0%

profile of v1, /device:TPU:1, one launch (start us, length us, event | category | flops | bytes accessed | tf_op | source)
XLA Modules:
  0.0 237.6 jit_solution(7161490932254744336)
XLA Ops:
  7.2 0.0 copy-start
  7.2 5.2 %convert_bitcast_fusion = bf16[64,1,16,1024]{3,0,2,1:T(8,128)(2,1)} fusion(bf16[1024,768]{1,0:T(8,128)(2,1)} %param.12, bf16[64,16,768]{2,1,0:T(8,128)(2,1)} %bitcast.137), kind=kOutput, calls=%fused_computation.4 | convolution fusion | flops 1611661312 | bytes 5242880 | tf_op jit(solution)/shard_map/sjrf,jdf->sjrd/dot_general | solution.py:39
  12.4 4.1 %reshape.179 = bf16[16,4,16,1024]{3,1,0,2:T(4,128)(2,1)} reshape(bf16[64,1,16,1024]{3,0,2,1:T(8,128)(2,1)} %convert_bitcast_fusion) | data formatting | bytes 4194304 | tf_op jit(solution)/shard_map/reshape | solution.py:40
  16.5 3.6 %copy.56 = bf16[16,4,16,1024]{3,0,2,1:T(8,128)(2,1)} copy(bf16[16,4,16,1024]{3,1,0,2:T(4,128)(2,1)} %reshape.179) | data formatting | bytes 4194304 | tf_op jit(solution)/shard_map/reshape | solution.py:40
  20.1 5.0 %all-to-all-start = ((bf16[16,4,16,1024]{3,0,2,1:T(8,128)(2,1)}), bf16[16,4,16,1024]{3,0,2,1:T(8,128)(2,1)}, u32[]{:S(2)}, u32[]{:S(2)}) async-start(bf16[16,4,16,1024]{3,0,2,1:T(8,128)(2,1)} %copy.56), calls=%async_computation | async-start | bytes 4194304 | tf_op jit(solution)/shard_map/all_to_all | solution.py:41
  25.1 0.0 reduce-scatter.2.cloned.1.call-start
  25.1 0.0 copy-done.4
  25.1 0.1 copy.42
  25.2 0.1 eq.49
  25.3 0.1 eq.53
  25.4 0.0 copy-done.5
  25.4 37.6 %all-gather.1 = f32[2048,4]{0,1:T(4,128)S(1)} all-gather(f32[128,4]{0,1:T(4,128)S(1)} %copy-done.5), channel_id=3, replica_groups=mesh['dp'=16,'ez'=16,'ex'=4] {'ez'}, dimensions={0}, use_global_device_ids=true | all-gather | bytes 34816 | tf_op jit(solution)/shard_map/all_gather | solution.py:55
  63.1 1.4 copy.58
  64.5 0.1 copy.47
  64.6 1.2 reduce-window.10
  65.8 0.2 slice_reduce_fusion
  66.1 0.1 fusion.17
  66.2 0.1 sub.47
  66.3 0.1 fusion.24
  66.4 26.9 %all-gather = s32[2048,4]{1,0:T(8,128)S(1)} all-gather(s32[128,4]{1,0:T(8,128)S(1)} %fusion.24), channel_id=2, replica_groups=mesh['dp'=16,'ez'=16,'ex'=4] {'ez'}, dimensions={0}, use_global_device_ids=true | all-gather | bytes 34816 | tf_op jit(solution)/shard_map/all_gather | solution.py:54
  93.3 1.0 copy-done.1
  94.3 2.9 %fusion.4 = f32[16,128,4]{2,1,0:T(8,128)} fusion(f32[16,128,4]{2,1,0:T(8,128)} %bitcast.136, s32[16,128,4]{2,1,0:T(8,128)S(1)} %bitcast.134, s32[]{:T(128)S(6)} %axis_index.15), kind=kLoop, calls=%fused_computation.21 | loop fusion | flops 139264 | bytes 98308 | tf_op jit(solution)/shard_map/jit(_where)/select_n | solution.py:59
  97.2 1.5 copy.54
  98.7 2.6 %add_select_fusion.1 = s32[16,128,4]{2,1,0:T(8,128)} fusion(s32[16,128,4]{2,1,0:T(8,128)} %bitcast.135), kind=kLoop, calls=%fused_computation.15 | loop fusion | flops 90112 | bytes 65536 | tf_op jit(solution)/shard_map/jit(remainder)/select_n | solution.py:60
  101.4 1.5 copy.52
  102.9 0.4 select_reduce_fusion
  103.3 0.0 all-to-all-done
  103.3 2.7 %copy.57 = bf16[16,4,16,1024]{3,2,1,0:T(8,128)(2,1)S(1)} copy(bf16[16,4,16,1024]{3,0,2,1:T(8,128)(2,1)} %all-to-all-done) | data formatting | bytes 4194304 | tf_op jit(solution)/shard_map/all_to_all | solution.py:41
  106.0 1.3 fusion.20
  107.3 3.2 %add_convert_fusion = bf16[16,128,1024]{2,1,0:T(8,128)(2,1)} fusion(f32[16,128,1024]{2,1,0:T(8,128)S(1)} %fusion.20, bf16[16,64,1024]{2,1,0:T(8,128)(2,1)S(1)} %bitcast.132, f32[16,128,64]{1,2,0:T(8,128)S(1)} %select_reduce_fusion), kind=kOutput, calls=%fused_computation.2 | convolution fusion | flops 273154048 | bytes 15204352 | tf_op jit(solution)/shard_map/ztr,zrd->ztd/dot_general | solution.py:65
  110.6 0.0 reduce-scatter.2.cloned.1.call-update
  110.6 0.6 copy-done.7
  111.2 0.2 reduce-window.14
  111.4 0.0 copy-done.6
  111.4 0.7 fusion.42
  112.1 0.0 copy-done.3
  112.1 0.7 fusion.41
  112.8 0.1 convert_reduce_fusion
  112.9 10.0 %fusion.38 = s32[64]{0:T(128)S(1)} fusion(s32[64]{0:T(128)S(1)} %convert_reduce_fusion, s32[]{:T(128)} %bitcast.28, s32[]{:T(128)} %bitcast.16, s32[]{:T(128)} %bitcast.29, s32[]{:T(128)} %bitcast.17, s32[]{:T(128)} %bitcast.30, s32[]{:T(128)} %bitcast.18, s32[]{:T(128)} %bitcast.31, s32[]{:T(128)} %bitcast.19, s32[]{:T(128)} %bitcast.32, s32[]{:T(128)} %bitcast.20, ...), kind=kLoop, calls=%fused_computation.89 | loop fusion | flops 1984 | bytes 576 | tf_op jit(solution)/shard_map/select_n | solution.py:81
  122.9 68.0 %reduce-scatter.2.cloned.1.call-done = bf16[128,1024]{1,0:T(8,128)(2,1)} async-done(((bf16[2048,1024]{1,0:T(8,128)(2,1)}), bf16[128,1024]{1,0:T(8,128)(2,1)}) %reduce-scatter.2.cloned.1.call-update) | async-done | bytes 262160 | tf_op jit(solution)/shard_map/reduce_scatter | solution.py:67
  190.9 2.3 scatter_custom_fusion
  193.1 0.1 reshape.185
  193.2 34.1 %all_to_all.10 = bf16[16,12,1024]{2,1,0:T(8,128)(2,1)} all-to-all(bf16[16,12,1024]{2,1,0:T(8,128)(2,1)S(1)} %reshape.185), channel_id=1, replica_groups=mesh['dp'=16,'ez'=16,'ex'=4] {'dp'}, dimensions={0} | all-to-all | bytes 786432 | tf_op jit(solution)/shard_map/all_to_all | solution.py:82
  227.4 1.1 reshape.186
  228.5 0.0 copy-start.2
  228.5 0.7 convolution_convert_fusion
  229.2 0.3 copy-done.2
  229.5 1.2 fusion.12
  (16 shorter events, 0.1 us)
Async XLA Ops:
  7.2 221.3 %copy-start = (bf16[1024,1280]{1,0:T(8,128)(2,1)S(1)}, bf16[1024,1280]{1,0:T(8,128)(2,1)}, u32[]{:S(2)}) copy-start(bf16[1024,1280]{1,0:T(8,128)(2,1)} %param.13) | copy-start | bytes 7864324
  20.1 5.0 %copy-start.4 = (s32[128,4]{0,1:T(4,128)S(1)}, s32[128,4]{0,1:T(4,128)}, u32[]{:S(2)}) copy-start(s32[128,4]{0,1:T(4,128)} %param.9) | copy-start | bytes 6148
  20.1 5.3 %copy-start.5 = (f32[128,4]{0,1:T(4,128)S(1)}, f32[128,4]{0,1:T(4,128)}, u32[]{:S(2)}) copy-start(f32[128,4]{0,1:T(4,128)} %param.10) | copy-start | bytes 6148
  20.1 83.2 %all-to-all-start = ((bf16[16,4,16,1024]{3,0,2,1:T(8,128)(2,1)}), bf16[16,4,16,1024]{3,0,2,1:T(8,128)(2,1)}, u32[]{:S(2)}, u32[]{:S(2)}) async-start(bf16[16,4,16,1024]{3,0,2,1:T(8,128)(2,1)} %copy.56), calls=%async_computation | async-start | bytes 4194304 | tf_op jit(solution)/shard_map/all_to_all | solution.py:41
  25.1 165.8 %reduce-scatter.2.cloned.1.call-start = ((), (), s32[]{:S(2)}) async-start(), calls=%async_computation.3 | async-start | bytes 4456448 | tf_op jit(solution)/shard_map/reduce_scatter | solution.py:67
  93.3 1.0 copy-start.1
  110.6 0.7 copy-start.7
  110.6 0.8 copy-start.6
  110.6 1.5 copy-start.3
  228.5 1.0 copy-start.2
Sparse Core Ops, SparseCore 0:
  110.7 80.0 reduce-scatter.1

commit v2 on v0

--- a/solution.py
+++ b/solution.py
@@ -34,6 +34,8 @@
     outgoing = jnp.einsum("sjrf,jdf->sjrd", incoming, weights, preferred_element_type=jnp.float32)
     outgoing = outgoing.astype(jnp.bfloat16).reshape(groups, slot_count, D)
     returned = lax.all_to_all(outgoing, "expert", split_axis=0, concat_axis=0, tiled=True)
+    returned = returned.reshape(groups * slot_count, D)
+
     token_count, top_count = expert_ids.shape
     flat_ids = expert_ids.reshape(-1)
     onehot = (flat_ids[:, None] == jnp.arange(experts_all, dtype=jnp.int32)[None, :]).astype(
@@ -41,10 +43,10 @@
     )
     route_rank = jnp.sum(jnp.cumsum(onehot, axis=0) * onehot, axis=1) - 1
     target = flat_ids // exp_dev * slot_count + flat_ids % exp_dev * capacity_each + route_rank
-    picked = returned.reshape(groups * slot_count, D)[target].reshape(token_count, top_count, D)
-    token_grad = jnp.sum(route_weight[:, :, None] * picked.astype(jnp.float32), axis=1).astype(
-        jnp.bfloat16
-    )
+    slots = jnp.arange(groups * slot_count, dtype=jnp.int32)
+    hits = target.reshape(token_count, top_count)[:, :, None] == slots[None, None, :]
+    mix = jnp.sum(jnp.where(hits, route_weight[:, :, None], 0.0), axis=1)
+
     positions = audio_pos[0]
     lengths = span_lengths[0]
     owners = span_owner[0]
@@ -56,8 +58,20 @@
     span_of = jnp.sum((audio_index[:, None] >= starts[None, :]).astype(jnp.int32), axis=1) - 1
     offset = audio_index - starts[span_of]
     place_at = owners[span_of] * span_cap + offset
-    audio_rows = token_grad[positions]
-    parcel = jnp.zeros((peer_count * span_cap, D), jnp.bfloat16).at[place_at].set(audio_rows)
+    parcel_rows = jnp.arange(peer_count * span_cap, dtype=jnp.int32)
+    lands = place_at[None, :] == parcel_rows[:, None]
+    token_of = jnp.sum(jnp.where(lands, positions[None, :] + 1, 0), axis=1) - 1
+    parcel_mix = jnp.where((token_of >= 0)[:, None], mix[jnp.maximum(token_of, 0)], 0.0)
+
+    all_mix = jnp.concatenate([mix, parcel_mix], axis=0)
+    mix_hi = all_mix.astype(jnp.bfloat16)
+    mix_lo = (all_mix - mix_hi.astype(jnp.float32)).astype(jnp.bfloat16)
+    summed = jnp.dot(mix_hi, returned, preferred_element_type=jnp.float32)
+    summed = summed + jnp.dot(mix_lo, returned, preferred_element_type=jnp.float32)
+    summed = summed.astype(jnp.bfloat16)
+    token_grad = summed[:token_count]
+    parcel = summed[token_count:]
+
     arrived_rows = lax.all_to_all(
         parcel.reshape(peer_count, span_cap, D), "dp", split_axis=0, concat_axis=0, tiled=True
     )

time: 173 us -> 166 us (0.960)
  blocking collectives: 30.4 us -> 0 us
  starting transfers between devices: 23.2 us -> 36.5 us
  waiting for transfers between devices: 80.9 us -> 92.2 us
  local copies, waits for them, and re-layouts: 16.5 us -> 10.2 us
  matrix products: 4.54 us -> 9.74 us
    all_to_all x1 -> x0, blocking collectives: 30.4 us -> none  [body(): lax.all_to_all(parcel.reshape(peer_count, span_cap, D), 'dp', split_axis=...]
    all_to_all x0 -> x1, waiting for transfers between devices: none -> 15.5 us  [body(): lax.all_to_all(parcel.reshape(peer_count, span_cap, D), 'dp', split_axis=...]
    all_to_all x0 -> x1, starting transfers between devices: none -> 13.3 us  [body(): lax.all_to_all(parcel.reshape(peer_count, span_cap, D), 'dp', split_axis=...]
    add x0 -> x1, other arithmetic: none -> 9.95 us  [body(): place_at = owners[span_of] * span_cap + offset]
    select_n x3 -> x1, other arithmetic: 9.96 us -> 2.13 us  [body(): jnp.where((token_of >= 0)[:, None], mix[jnp.maximum(token_of, 0)], 0.0)]
    dot_general x0 -> x2, matrix products: none -> 5.2 us  [the longest x1 2.74 us: body(): summed = jnp.dot(mix_hi, returned, preferred_element_type=jnp.float32)]
    all_to_all x1, waiting for transfers between devices: 80.9 us -> 76.7 us  [body(): lax.all_to_all(outgoing, 'expert', split_axis=0, concat_axis=0, tiled=True)]
    gather x1, local copies, waits for them, and re-layouts: 5.35 us -> 1.8 us  [body(): mix[jnp.maximum(token_of, 0)]]
  transfers between devices with their start and end apart: 1 -> 2, of which waited for: 1 -> 2; matrix products, arithmetic and copies ran while one was open for 8% -> 12% of each run, Pallas kernels for 0% -> 0%
where the time goes in v2:
time: 166 us; the launch traced here: 165 us
  waiting for transfers between devices  92.2 us (56%)
  starting transfers between devices  36.5 us (22%)
  other arithmetic  15.4 us (9%)
  local copies, waits for them, and re-layouts  10.2 us (6%)
  matrix products  9.74 us (6%)
    all_to_all x1, waiting for transfers between devices, body(): lax.all_to_all(outgoing, 'expert', split_axis=0, concat_axis=0, tiled=True)  76.7 us
    all_to_all x1, starting transfers between devices, body(): lax.all_to_all(outgoing, 'expert', split_axis=0, concat_axis=0, tiled=True)  23.2 us
    all_to_all x1, waiting for transfers between devices, body(): lax.all_to_all(parcel.reshape(peer_count, span_cap, D), 'dp', split_axis=...  15.5 us
    all_to_all x1, starting transfers between devices, body(): lax.all_to_all(parcel.reshape(peer_count, span_cap, D), 'dp', split_axis=...  13.3 us
    add x1, other arithmetic, body(): place_at = owners[span_of] * span_cap + offset  9.95 us
    dot_general x1, matrix products, body(): jnp.einsum('sjrf,jdf->sjrd', incoming, weights, preferred_element_type=jn...  3.86 us
  transfers between devices with their start and end apart: 2, of which 2 were waited for; matrix products, arithmetic and copies ran while one was open for 12% of the time, Pallas kernels for 0%

profile of v2, /device:TPU:1, one launch (start us, length us, event | category | flops | bytes accessed | tf_op | source)
XLA Modules:
  0.0 164.9 jit_solution(1187557646230516539)
XLA Ops:
  0.6 0.0 copy-start
  0.6 3.9 %convert_bitcast_fusion = bf16[64,16,1024]{2,0,1:T(8,128)(2,1)S(1)} fusion(bf16[1024,768]{1,0:T(8,128)(2,1)} %param.12, bf16[64,16,768]{2,1,0:T(8,128)(2,1)} %bitcast.90), kind=kOutput, calls=%fused_computation.2 | convolution fusion | flops 1611661312 | bytes 5242880 | tf_op jit(solution)/shard_map/sjrf,jdf->sjrd/dot_general | solution.py:34
  4.5 2.4 %copy.43 = bf16[64,16,1024]{2,1,0:T(8,128)(2,1)} copy(bf16[64,16,1024]{2,0,1:T(8,128)(2,1)S(1)} %convert_bitcast_fusion) | data formatting | bytes 4194304 | tf_op jit(solution)/shard_map/reshape | solution.py:35
  7.0 0.0 copy-start.5
  7.0 0.0 copy-start.7
  7.0 0.0 copy-start.4
  7.0 0.0 copy-start.8
  7.0 0.0 copy-start.6
  7.0 23.2 %all-to-all-start = ((bf16[64,16,1024]{2,1,0:T(8,128)(2,1)}), bf16[64,16,1024]{2,1,0:T(8,128)(2,1)}, u32[]{:S(2)}, u32[]{:S(2)}) async-start(bf16[64,16,1024]{2,1,0:T(8,128)(2,1)} %copy.43), calls=%async_computation | async-start | bytes 4194304 | tf_op jit(solution)/shard_map/all_to_all | solution.py:36
  30.2 0.0 copy-done.5
  30.2 0.1 copy.38
  30.3 0.1 eq.53
  30.4 0.1 eq.57
  30.5 1.2 reduce-window.10
  31.7 0.2 slice_reduce_fusion
  32.0 0.1 fusion.15
  32.1 0.1 sub.37
  32.3 0.1 copy.41
  32.3 0.0 copy-done.7
  32.3 0.2 reduce-window.14
  32.5 0.7 fusion.26
  33.2 0.0 copy-done.4
  33.2 0.7 fusion.25
  33.9 0.1 convert_reduce_fusion
  34.0 0.0 copy-done.8
  34.0 9.9 %fusion.19 = s32[64]{0:T(128)S(1)} fusion(s32[64]{0:T(128)S(1)} %convert_reduce_fusion, s32[]{:T(128)} %bitcast.19, s32[]{:T(128)} %bitcast.8, s32[]{:T(128)} %bitcast.20, s32[]{:T(128)} %bitcast.9, s32[]{:T(128)} %bitcast.21, s32[]{:T(128)} %bitcast.10, s32[]{:T(128)} %bitcast.22, s32[]{:T(128)} %bitcast.11, s32[]{:T(128)} %bitcast.23, s32[]{:T(128)} %bitcast.12, ...), kind=kLoop, calls=%fused_computation.60 | loop fusion | flops 1792 | bytes 576 | tf_op jit(solution)/shard_map/add | solution.py:60
  43.9 0.1 select_reduce_fusion.1
  44.1 0.0 copy-done.6
  44.1 0.3 select_reduce_fusion
  44.4 1.8 %gather_fusion = f32[192,1024]{1,0:T(8,128)} fusion(f32[128,1024]{1,0:T(8,128)S(1)} %select_reduce_fusion, s32[1024]{0:T(1024)S(1)} %pad_clamp_fusion), kind=kCustom, calls=%fused_computation | custom fusion | bytes 1573632 | tf_op jit(solution)/shard_map/gather | solution.py:64
  46.2 2.1 %broadcast_select_fusion = f32[192,1024]{1,0:T(8,128)} fusion(f32[192,1024]{1,0:T(8,128)} %gather_fusion, pred[192]{0:T(512)(128)(4,1)S(1)} %add_compare_fusion), kind=kLoop, calls=%fused_computation.25 | loop fusion | flops 196608 | bytes 1573056 | tf_op jit(solution)/shard_map/jit(_where)/select_n | solution.py:64
  48.3 76.7 %all-to-all-done = bf16[64,16,1024]{2,1,0:T(8,128)(2,1)} async-done(((bf16[64,16,1024]{2,1,0:T(8,128)(2,1)}), bf16[64,16,1024]{2,1,0:T(8,128)(2,1)}, u32[]{:S(2)}, u32[]{:S(2)}) %all-to-all-start) | async-done | bytes 2097184 | tf_op jit(solution)/shard_map/all_to_all | solution.py:36
  125.0 0.0 copy-start.1
  125.0 2.7 %fusion.12 = f32[320,1024]{1,0:T(8,128)S(1)} fusion(bf16[1024,1024]{1,0:T(8,128)(2,1)} %bitcast.33, f32[192,1024]{1,0:T(8,128)} %broadcast_select_fusion, f32[128,1024]{1,0:T(8,128)S(1)} %select_reduce_fusion), kind=kOutput, calls=%fused_computation.24 | convolution fusion | flops 672399360 | bytes 4718592 | tf_op jit(solution)/shard_map/dot_general | solution.py:69
  127.8 0.0 copy-done.1
  127.8 2.5 %fusion.2 = bf16[320,1024]{1,0:T(8,128)(2,1)S(1)} fusion(f32[320,1024]{1,0:T(8,128)S(1)} %fusion.12, bf16[1024,1024]{1,0:T(8,128)(2,1)} %bitcast.33, f32[192,1024]{1,0:T(8,128)S(1)} %copy-done.1, f32[128,1024]{1,0:T(8,128)S(1)} %select_reduce_fusion), kind=kOutput, calls=%fused_computation.12 | convolution fusion | flops 673382400 | bytes 5373952 | tf_op jit(solution)/shard_map/dot_general | solution.py:70
  130.3 0.0 copy-start.2
  130.3 0.8 copy-done.2
  131.1 0.9 reshape.120
  132.0 13.3 %all-to-all-start.1 = ((bf16[16,12,1024]{2,1,0:T(8,128)(2,1)}), bf16[16,12,1024]{2,1,0:T(8,128)(2,1)S(1)}, u32[]{:S(2)}, u32[]{:S(2)}) async-start(bf16[16,12,1024]{2,1,0:T(8,128)(2,1)} %reshape.120), calls=%async_computation.1 | async-start | bytes 1048576 | tf_op jit(solution)/shard_map/all_to_all | solution.py:75
  145.3 1.7 %slice.46 = bf16[128,1024]{1,0:T(8,128)(2,1)} slice(bf16[320,1024]{1,0:T(8,128)(2,1)} %copy-done.2), slice={[0:128], [0:1024]} | slice | bytes 524288 | tf_op jit(solution)/shard_map/slice | solution.py:72
  146.9 15.5 %all-to-all-done.1 = bf16[16,12,1024]{2,1,0:T(8,128)(2,1)S(1)} async-done(((bf16[16,12,1024]{2,1,0:T(8,128)(2,1)}), bf16[16,12,1024]{2,1,0:T(8,128)(2,1)S(1)}, u32[]{:S(2)}, u32[]{:S(2)}) %all-to-all-start.1) | async-done | bytes 393248 | tf_op jit(solution)/shard_map/all_to_all | solution.py:75
  162.5 0.1 reshape.121
  162.6 0.0 copy-done
  162.6 0.0 copy-start.3
  162.6 0.7 convolution_convert_fusion
  163.3 0.3 copy-done.3
  163.6 1.2 fusion.11
  (12 shorter events, 0.1 us)
Async XLA Ops:
  0.6 161.9 %copy-start = (bf16[1024,1280]{1,0:T(8,128)(2,1)S(1)}, bf16[1024,1280]{1,0:T(8,128)(2,1)}, u32[]{:S(2)}) copy-start(bf16[1024,1280]{1,0:T(8,128)(2,1)} %param.13) | copy-start | bytes 7864324
  7.0 23.2 %copy-start.5 = (s32[128,4]{0,1:T(4,128)S(1)}, s32[128,4]{0,1:T(4,128)}, u32[]{:S(2)}) copy-start(s32[128,4]{0,1:T(4,128)} %param.9) | copy-start | bytes 6148
  7.0 25.4 %copy-start.7 = (s32[1,8]{1,0:T(1,128)S(1)}, s32[1,8]{1,0:T(1,128)}, u32[]{:S(2)}) copy-start(s32[1,8]{1,0:T(1,128)} %param.15) | copy-start | bytes 100
  7.0 26.3 %copy-start.4 = (s32[1,8]{1,0:T(1,128)S(1)}, s32[1,8]{1,0:T(1,128)}, u32[]{:S(2)}) copy-start(s32[1,8]{1,0:T(1,128)} %param.16) | copy-start | bytes 100
  7.0 27.0 %copy-start.8 = (s32[1,64]{1,0:T(1,128)S(1)}, s32[1,64]{1,0:T(1,128)}, u32[]{:S(2)}) copy-start(s32[1,64]{1,0:T(1,128)} %param.17) | copy-start | bytes 772
  7.0 37.1 %copy-start.6 = (f32[128,4]{0,1:T(4,128)S(1)}, f32[128,4]{0,1:T(4,128)}, u32[]{:S(2)}) copy-start(f32[128,4]{0,1:T(4,128)} %param.10) | copy-start | bytes 6148
  7.0 118.0 %all-to-all-start = ((bf16[64,16,1024]{2,1,0:T(8,128)(2,1)}), bf16[64,16,1024]{2,1,0:T(8,128)(2,1)}, u32[]{:S(2)}, u32[]{:S(2)}) async-start(bf16[64,16,1024]{2,1,0:T(8,128)(2,1)} %copy.43), calls=%async_computation | async-start | bytes 4194304 | tf_op jit(solution)/shard_map/all_to_all | solution.py:36
  125.0 2.8 %copy-start.1 = (f32[192,1024]{1,0:T(8,128)S(1)}, f32[192,1024]{1,0:T(8,128)}, u32[]{:S(2)}) copy-start(f32[192,1024]{1,0:T(8,128)} %broadcast_select_fusion) | copy-start | bytes 2359300
  130.3 0.8 copy-start.2
  132.0 30.5 %all-to-all-start.1 = ((bf16[16,12,1024]{2,1,0:T(8,128)(2,1)}), bf16[16,12,1024]{2,1,0:T(8,128)(2,1)S(1)}, u32[]{:S(2)}, u32[]{:S(2)}) async-start(bf16[16,12,1024]{2,1,0:T(8,128)(2,1)} %reshape.120), calls=%async_computation.1 | async-start | bytes 1048576 | tf_op jit(solution)/shard_map/all_to_all | solution.py:75
  162.6 1.0 copy-start.3

commit v3 on v2

--- a/solution.py
+++ b/solution.py
@@ -31,7 +31,14 @@
     hidden_width = gate_weight.shape[1]
     incoming = d_gate.reshape(groups, exp_dev, capacity_each, hidden_width)
     weights = gate_weight.reshape(exp_dev, D, hidden_width)
-    outgoing = jnp.einsum("sjrf,jdf->sjrd", incoming, weights, preferred_element_type=jnp.float32)
+    if exp_dev == 1:
+        outgoing = lax.dot_general(
+            d_gate, gate_weight, (((1,), (1,)), ((), ())), preferred_element_type=jnp.float32
+        )
+    else:
+        outgoing = jnp.einsum(
+            "sjrf,jdf->sjrd", incoming, weights, preferred_element_type=jnp.float32
+        )
     outgoing = outgoing.astype(jnp.bfloat16).reshape(groups, slot_count, D)
     returned = lax.all_to_all(outgoing, "expert", split_axis=0, concat_axis=0, tiled=True)
     returned = returned.reshape(groups * slot_count, D)
@@ -63,19 +70,20 @@
     token_of = jnp.sum(jnp.where(lands, positions[None, :] + 1, 0), axis=1) - 1
     parcel_mix = jnp.where((token_of >= 0)[:, None], mix[jnp.maximum(token_of, 0)], 0.0)
 
-    all_mix = jnp.concatenate([mix, parcel_mix], axis=0)
-    mix_hi = all_mix.astype(jnp.bfloat16)
-    mix_lo = (all_mix - mix_hi.astype(jnp.float32)).astype(jnp.bfloat16)
-    summed = jnp.dot(mix_hi, returned, preferred_element_type=jnp.float32)
-    summed = summed + jnp.dot(mix_lo, returned, preferred_element_type=jnp.float32)
-    summed = summed.astype(jnp.bfloat16)
-    token_grad = summed[:token_count]
-    parcel = summed[token_count:]
+    def combine(weights_f32):
+        hi = lax.optimization_barrier(weights_f32.astype(jnp.bfloat16))
+        lo = (weights_f32 - hi.astype(jnp.float32)).astype(jnp.bfloat16)
+        total = jnp.dot(hi, returned, preferred_element_type=jnp.float32)
+        total = total + jnp.dot(lo, returned, preferred_element_type=jnp.float32)
+        return total.astype(jnp.bfloat16)
+
+    parcel = combine(parcel_mix)
 
     arrived_rows = lax.all_to_all(
         parcel.reshape(peer_count, span_cap, D), "dp", split_axis=0, concat_axis=0, tiled=True
     )
     arrived_rows = arrived_rows.reshape(peer_count * span_cap, D)
+    token_grad = combine(mix)
     arrived = jnp.dot(arrived_rows, projector, preferred_element_type=jnp.float32).astype(
         jnp.bfloat16
     )

time: 166 us -> 166 us (level)
  matrix products: 9.74 us -> 15.8 us
  local copies, waits for them, and re-layouts: 10.2 us -> 7.29 us
  waiting for transfers between devices: 92.2 us -> 90.1 us
    dot_general x3 -> x5, matrix products: 9.06 us -> 15.1 us  [the longest x2 5.72 us: combine(): total = total + jnp.dot(lo, returned, preferred_element_type=jnp.float32)]
    all_to_all x1, waiting for transfers between devices: 15.5 us -> 12.5 us  [body(): lax.all_to_all(parcel.reshape(peer_count, span_cap, D), 'dp', split_axis=...]
    reshape x1 -> x0, local copies, waits for them, and re-layouts: 2.45 us -> none  [body(): outgoing = outgoing.astype(jnp.bfloat16).reshape(groups, slot_count, D)]
    select_n x1 -> x0, other arithmetic: 2.13 us -> none  [body(): jnp.where((token_of >= 0)[:, None], mix[jnp.maximum(token_of, 0)], 0.0)]
    slice x3 -> x1, local copies, waits for them, and re-layouts: 1.93 us -> 0.23 us  [the longest x1 1.67 us: body(): token_grad = summed[:token_count]]
  transfers between devices with their start and end apart: 2 -> 2, of which waited for: 2 -> 2; matrix products, arithmetic and copies ran while one was open for 12% -> 13% of each run, Pallas kernels for 0% -> 0%
where the time goes in v3:
time: 166 us; the launch traced here: 165 us
  waiting for transfers between devices  90.1 us (54%)
  starting transfers between devices  36.5 us (22%)
  matrix products  15.8 us (10%)
  other arithmetic  14.5 us (9%)
  local copies, waits for them, and re-layouts  7.29 us (4%)
    all_to_all x1, waiting for transfers between devices, body(): lax.all_to_all(outgoing, 'expert', split_axis=0, concat_axis=0, tiled=True)  77.6 us
    all_to_all x1, starting transfers between devices, body(): lax.all_to_all(outgoing, 'expert', split_axis=0, concat_axis=0, tiled=True)  23.2 us
    all_to_all x1, starting transfers between devices, body(): lax.all_to_all(parcel.reshape(peer_count, span_cap, D), 'dp', split_axis=...  13.3 us
    all_to_all x1, waiting for transfers between devices, body(): lax.all_to_all(parcel.reshape(peer_count, span_cap, D), 'dp', split_axis=...  12.5 us
    add x1, other arithmetic, body(): place_at = owners[span_of] * span_cap + offset  9.95 us
    dot_general x2, matrix products, combine(): total = total + jnp.dot(lo, returned, preferred_element_type=jnp.float32)  5.72 us
    dot_general x1, matrix products, body(): lax.dot_general(d_gate, gate_weight, (((1,), (1,)), ((), ())), preferred_...  5.15 us
    dot_general x2, matrix products, combine(): total = jnp.dot(hi, returned, preferred_element_type=jnp.float32)  4.27 us
  transfers between devices with their start and end apart: 2, of which 2 were waited for; matrix products, arithmetic and copies ran while one was open for 13% of the time, Pallas kernels for 0%

profile of v3, /device:TPU:1, one launch (start us, length us, event | category | flops | bytes accessed | tf_op | source)
XLA Modules:
  0.0 165.0 jit_solution(5255548534909617671)
XLA Ops:
  0.6 0.0 copy-start
  0.6 5.1 %convolution_convert_fusion.1 = bf16[1024,1024]{1,0:T(8,128)(2,1)} fusion(bf16[1024,768]{1,0:T(8,128)(2,1)} %param.11, bf16[1024,768]{1,0:T(8,128)(2,1)} %param.12), kind=kOutput, calls=%fused_computation.4 | convolution fusion | flops 1611661312 | bytes 5242880 | tf_op jit(solution)/shard_map/dot_general | solution.py:35
  5.8 0.0 copy-start.4
  5.8 0.0 copy-start.6
  5.8 0.0 copy-start.3
  5.8 0.0 copy-start.7
  5.8 0.0 copy-start.5
  5.8 23.2 %all-to-all-start = ((bf16[64,16,1024]{2,1,0:T(8,128)(2,1)}), bf16[64,16,1024]{2,1,0:T(8,128)(2,1)}, u32[]{:S(2)}, u32[]{:S(2)}) async-start(bf16[64,16,1024]{2,1,0:T(8,128)(2,1)} %bitcast.87), calls=%async_computation | async-start | bytes 4194304 | tf_op jit(solution)/shard_map/all_to_all | solution.py:43
  29.0 0.0 copy-done.4
  29.0 0.1 copy.25
  29.1 0.1 eq.53
  29.2 0.1 eq.57
  29.4 1.2 reduce-window.10
  30.6 0.2 slice_reduce_fusion
  30.8 0.1 fusion.13
  31.0 0.1 sub.40
  31.1 0.1 copy.28
  31.2 0.0 copy-done.6
  31.2 0.2 reduce-window.14
  31.4 0.7 fusion.23
  32.1 0.0 copy-done.3
  32.1 0.7 fusion.22
  32.7 0.1 convert_reduce_fusion
  32.8 0.0 copy-done.7
  32.8 9.9 %fusion.17 = s32[64]{0:T(128)S(1)} fusion(s32[64]{0:T(128)S(1)} %convert_reduce_fusion, s32[]{:T(128)} %bitcast.21, s32[]{:T(128)} %bitcast.10, s32[]{:T(128)} %bitcast.22, s32[]{:T(128)} %bitcast.11, s32[]{:T(128)} %bitcast.23, s32[]{:T(128)} %bitcast.12, s32[]{:T(128)} %bitcast.24, s32[]{:T(128)} %bitcast.13, s32[]{:T(128)} %bitcast.25, s32[]{:T(128)} %bitcast.14, ...), kind=kLoop, calls=%fused_computation.60 | loop fusion | flops 1792 | bytes 576 | tf_op jit(solution)/shard_map/add | solution.py:67
  42.8 0.1 select_reduce_fusion.1
  42.9 0.0 copy-done.5
  42.9 0.3 select_reduce_fusion
  43.2 1.8 %gather_fusion = f32[192,1024]{1,0:T(8,128)} fusion(f32[128,1024]{1,0:T(8,128)S(1)} %select_reduce_fusion, s32[1024]{0:T(1024)S(1)} %pad_clamp_fusion), kind=kCustom, calls=%fused_computation | custom fusion | bytes 1573632 | tf_op jit(solution)/shard_map/gather | solution.py:71
  45.0 1.2 select_convert_fusion
  46.3 77.6 %all-to-all-done = bf16[64,16,1024]{2,1,0:T(8,128)(2,1)} async-done(((bf16[64,16,1024]{2,1,0:T(8,128)(2,1)}), bf16[64,16,1024]{2,1,0:T(8,128)(2,1)}, u32[]{:S(2)}, u32[]{:S(2)}) %all-to-all-start) | async-done | bytes 2097184 | tf_op jit(solution)/shard_map/all_to_all | solution.py:43
  123.9 0.0 copy-start.1
  123.9 2.2 %fusion.25 = f32[192,1024]{1,0:T(8,128)S(1)} fusion(bf16[192,1024]{1,0:T(8,128)(2,1)S(1)} %select_convert_fusion, bf16[1024,1024]{1,0:T(8,128)(2,1)} %bitcast.2), kind=kOutput, calls=%fused_computation.71 | convolution fusion | flops 402653184 | bytes 3276800 | tf_op jit(solution)/shard_map/dot_general | solution.py:76
  126.1 0.0 copy-done.1
  126.1 3.0 %fusion = bf16[192,1024]{1,0:T(8,128)(2,1)} fusion(f32[192,1024]{1,0:T(8,128)S(1)} %fusion.25, bf16[1024,1024]{1,0:T(8,128)(2,1)} %bitcast.2, bf16[192,1024]{1,0:T(8,128)(2,1)S(1)} %select_convert_fusion, f32[192,1024]{1,0:T(8,128)S(1)} %copy-done.1, pred[192]{0:T(512)(128)(4,1)S(1)} %add_compare_fusion), kind=kOutput, calls=%fused_computation.10 | convolution fusion | flops 403832832 | bytes 4456640 | tf_op jit(solution)/shard_map/dot_general | solution.py:77
  129.1 1.9 %reshape.109 = bf16[16,12,1024]{2,1,0:T(8,128)(2,1)} reshape(bf16[192,1024]{1,0:T(8,128)(2,1)} %fusion) | data formatting | bytes 786432 | tf_op jit(solution)/shard_map/reshape | solution.py:83
  131.0 13.3 %all-to-all-start.1 = ((bf16[16,12,1024]{2,1,0:T(8,128)(2,1)}), bf16[16,12,1024]{2,1,0:T(8,128)(2,1)}, u32[]{:S(2)}, u32[]{:S(2)}) async-start(bf16[16,12,1024]{2,1,0:T(8,128)(2,1)} %reshape.109), calls=%async_computation.1 | async-start | bytes 1048576 | tf_op jit(solution)/shard_map/all_to_all | solution.py:82
  144.3 2.0 %fusion.24 = f32[128,1024]{1,0:T(8,128)S(1)} fusion(bf16[128,1024]{1,0:T(8,128)(2,1)S(1)} %convert_element_type.48, bf16[1024,1024]{1,0:T(8,128)(2,1)} %bitcast.2), kind=kOutput, calls=%fused_computation.70 | convolution fusion | flops 268435456 | bytes 2883584 | tf_op jit(solution)/shard_map/dot_general | solution.py:76
  146.4 2.7 %fusion.1 = bf16[128,1024]{1,0:T(8,128)(2,1)} fusion(f32[128,1024]{1,0:T(8,128)S(1)} %fusion.24, bf16[1024,1024]{1,0:T(8,128)(2,1)} %bitcast.2, f32[128,1024]{1,0:T(8,128)S(1)} %select_reduce_fusion, bf16[128,1024]{1,0:T(8,128)(2,1)S(1)} %convert_element_type.48), kind=kOutput, calls=%fused_computation.12 | convolution fusion | flops 269090816 | bytes 3670016 | tf_op jit(solution)/shard_map/dot_general | solution.py:77
  149.1 12.5 %all-to-all-done.1 = bf16[16,12,1024]{2,1,0:T(8,128)(2,1)} async-done(((bf16[16,12,1024]{2,1,0:T(8,128)(2,1)}), bf16[16,12,1024]{2,1,0:T(8,128)(2,1)}, u32[]{:S(2)}, u32[]{:S(2)}) %all-to-all-start.1) | async-done | bytes 393248 | tf_op jit(solution)/shard_map/all_to_all | solution.py:82
  161.6 1.1 reshape.110
  162.7 0.0 copy-done
  162.7 0.0 copy-start.2
  162.7 0.7 convolution_convert_fusion
  163.4 0.3 copy-done.2
  163.8 1.2 fusion.9
  (12 shorter events, 0.1 us)
Async XLA Ops:
  0.6 162.1 %copy-start = (bf16[1024,1280]{1,0:T(8,128)(2,1)S(1)}, bf16[1024,1280]{1,0:T(8,128)(2,1)}, u32[]{:S(2)}) copy-start(bf16[1024,1280]{1,0:T(8,128)(2,1)} %param.13) | copy-start | bytes 7864324
  5.8 23.2 %copy-start.4 = (s32[128,4]{0,1:T(4,128)S(1)}, s32[128,4]{0,1:T(4,128)}, u32[]{:S(2)}) copy-start(s32[128,4]{0,1:T(4,128)} %param.9) | copy-start | bytes 6148
  5.8 25.4 %copy-start.6 = (s32[1,8]{1,0:T(1,128)S(1)}, s32[1,8]{1,0:T(1,128)}, u32[]{:S(2)}) copy-start(s32[1,8]{1,0:T(1,128)} %param.15) | copy-start | bytes 100
  5.8 26.3 %copy-start.3 = (s32[1,8]{1,0:T(1,128)S(1)}, s32[1,8]{1,0:T(1,128)}, u32[]{:S(2)}) copy-start(s32[1,8]{1,0:T(1,128)} %param.16) | copy-start | bytes 100
  5.8 27.0 %copy-start.7 = (s32[1,64]{1,0:T(1,128)S(1)}, s32[1,64]{1,0:T(1,128)}, u32[]{:S(2)}) copy-start(s32[1,64]{1,0:T(1,128)} %param.17) | copy-start | bytes 772
  5.8 37.1 %copy-start.5 = (f32[128,4]{0,1:T(4,128)S(1)}, f32[128,4]{0,1:T(4,128)}, u32[]{:S(2)}) copy-start(f32[128,4]{0,1:T(4,128)} %param.10) | copy-start | bytes 6148
  5.8 118.0 %all-to-all-start = ((bf16[64,16,1024]{2,1,0:T(8,128)(2,1)}), bf16[64,16,1024]{2,1,0:T(8,128)(2,1)}, u32[]{:S(2)}, u32[]{:S(2)}) async-start(bf16[64,16,1024]{2,1,0:T(8,128)(2,1)} %bitcast.87), calls=%async_computation | async-start | bytes 4194304 | tf_op jit(solution)/shard_map/all_to_all | solution.py:43
  123.9 2.3 %copy-start.1 = (f32[192,1024]{1,0:T(8,128)S(1)}, f32[192,1024]{1,0:T(8,128)}, u32[]{:S(2)}) copy-start(f32[192,1024]{1,0:T(8,128)} %gather_fusion) | copy-start | bytes 2359300
  131.0 30.6 %all-to-all-start.1 = ((bf16[16,12,1024]{2,1,0:T(8,128)(2,1)}), bf16[16,12,1024]{2,1,0:T(8,128)(2,1)}, u32[]{:S(2)}, u32[]{:S(2)}) async-start(bf16[16,12,1024]{2,1,0:T(8,128)(2,1)} %reshape.109), calls=%async_computation.1 | async-start | bytes 1048576 | tf_op jit(solution)/shard_map/all_to_all | solution.py:82
  162.7 1.0 copy-start.2

commit v4 on v3

--- a/solution.py
+++ b/solution.py
@@ -64,8 +64,9 @@
     audio_index = jnp.arange(audio_count, dtype=jnp.int32)
     span_of = jnp.sum((audio_index[:, None] >= starts[None, :]).astype(jnp.int32), axis=1) - 1
     offset = audio_index - starts[span_of]
-    place_at = owners[span_of] * span_cap + offset
-    parcel_rows = jnp.arange(peer_count * span_cap, dtype=jnp.int32)
+    block_rows = -(-span_cap // 16) * 16
+    place_at = owners[span_of] * block_rows + offset
+    parcel_rows = jnp.arange(peer_count * block_rows, dtype=jnp.int32)
     lands = place_at[None, :] == parcel_rows[:, None]
     token_of = jnp.sum(jnp.where(lands, positions[None, :] + 1, 0), axis=1) - 1
     parcel_mix = jnp.where((token_of >= 0)[:, None], mix[jnp.maximum(token_of, 0)], 0.0)
@@ -73,24 +74,24 @@
     def combine(weights_f32):
         hi = lax.optimization_barrier(weights_f32.astype(jnp.bfloat16))
         lo = (weights_f32 - hi.astype(jnp.float32)).astype(jnp.bfloat16)
-        total = jnp.dot(hi, returned, preferred_element_type=jnp.float32)
-        total = total + jnp.dot(lo, returned, preferred_element_type=jnp.float32)
-        return total.astype(jnp.bfloat16)
+        rows = weights_f32.shape[0]
+        total = jnp.dot(jnp.concatenate([hi, lo]), returned, preferred_element_type=jnp.float32)
+        return (total[:rows] + total[rows:]).astype(jnp.bfloat16)
 
     parcel = combine(parcel_mix)
 
     arrived_rows = lax.all_to_all(
-        parcel.reshape(peer_count, span_cap, D), "dp", split_axis=0, concat_axis=0, tiled=True
+        parcel.reshape(peer_count, block_rows, D), "dp", split_axis=0, concat_axis=0, tiled=True
     )
-    arrived_rows = arrived_rows.reshape(peer_count * span_cap, D)
+    arrived_rows = arrived_rows.reshape(peer_count * block_rows, D)
     token_grad = combine(mix)
     arrived = jnp.dot(arrived_rows, projector, preferred_element_type=jnp.float32).astype(
         jnp.bfloat16
     )
     gelu_factor = gelu_slope(enc_pre.astype(jnp.float32))
-    enc_grad = (lax.optimization_barrier(arrived).astype(jnp.float32) * gelu_factor).astype(
-        jnp.bfloat16
-    )
+    arrived = lax.optimization_barrier(arrived).reshape(peer_count, block_rows, -1)
+    arrived = arrived[:, :span_cap].reshape(peer_count * span_cap, -1)
+    enc_grad = (arrived.astype(jnp.float32) * gelu_factor).astype(jnp.bfloat16)
     return (token_grad, enc_grad)
 
 

time: 166 us -> 167 us (level)
  other arithmetic: 14.5 us -> 19.8 us
  matrix products: 15.8 us -> 12.5 us
    convert_element_type x1 -> x6, other arithmetic: 1.24 us -> 6.36 us  [the longest x2 3.6 us: body(): enc_grad = (arrived.astype(jnp.float32) * gelu_factor).astype(jnp.bfloat16)]
    dot_general x4 -> x2, matrix products: 9.99 us -> 5.47 us  [combine(): jnp.dot(jnp.concatenate([hi, lo]), returned, preferred_element_type=jnp.f...]
    reshape x2 -> x0, local copies, waits for them, and re-layouts: 3.02 us -> none  [the longest x1 1.89 us: body(): parcel.reshape(peer_count, span_cap, D)]
    convert_element_type x0 -> x1, local copies, waits for them, and re-layouts: none -> 2.4 us  [body(): enc_grad = (arrived.astype(jnp.float32) * gelu_factor).astype(jnp.bfloat16)]
    all_to_all x1, waiting for transfers between devices: 77.6 us -> 75.4 us  [body(): lax.all_to_all(outgoing, 'expert', split_axis=0, concat_axis=0, tiled=True)]
where the time goes in v4:
time: 167 us; the launch traced here: 166 us
  waiting for transfers between devices  89.5 us (54%)
  starting transfers between devices  36.5 us (22%)
  other arithmetic  19.8 us (12%)
  matrix products  12.5 us (7%)
  local copies, waits for them, and re-layouts  7.35 us (4%)
    all_to_all x1, waiting for transfers between devices, body(): lax.all_to_all(outgoing, 'expert', split_axis=0, concat_axis=0, tiled=True)  75.4 us
    all_to_all x1, starting transfers between devices, body(): lax.all_to_all(outgoing, 'expert', split_axis=0, concat_axis=0, tiled=True)  23.2 us
    all_to_all x1, waiting for transfers between devices, body(): lax.all_to_all(parcel.reshape(peer_count, block_rows, D), 'dp', split_axi...  14.1 us
    all_to_all x1, starting transfers between devices, body(): lax.all_to_all(parcel.reshape(peer_count, block_rows, D), 'dp', split_axi...  13.3 us
    add x1, other arithmetic, body(): place_at = owners[span_of] * block_rows + offset  9.95 us
    dot_general x2, matrix products, combine(): jnp.dot(jnp.concatenate([hi, lo]), returned, preferred_element_type=jnp.f...  5.47 us
    dot_general x1, matrix products, body(): lax.dot_general(d_gate, gate_weight, (((1,), (1,)), ((), ())), preferred_...  5.15 us
    convert_element_type x2, other arithmetic, body(): enc_grad = (arrived.astype(jnp.float32) * gelu_factor).astype(jnp.bfloat16)  3.6 us
  transfers between devices with their start and end apart: 2, of which 2 were waited for; matrix products, arithmetic and copies ran while one was open for 13% of the time, Pallas kernels for 0%

profile of v4, /device:TPU:1, one launch (start us, length us, event | category | flops | bytes accessed | tf_op | source)
XLA Modules:
  0.0 166.5 jit_solution(8286206328269259076)
XLA Ops:
  0.6 0.0 copy-start
  0.6 5.1 %convolution_convert_fusion.1 = bf16[1024,1024]{1,0:T(8,128)(2,1)} fusion(bf16[1024,768]{1,0:T(8,128)(2,1)} %param.11, bf16[1024,768]{1,0:T(8,128)(2,1)} %param.12), kind=kOutput, calls=%fused_computation.4 | convolution fusion | flops 1611661312 | bytes 5242880 | tf_op jit(solution)/shard_map/dot_general | solution.py:35
  5.8 0.0 copy-start.5
  5.8 0.0 copy-start.7
  5.8 0.0 copy-start.4
  5.8 0.0 copy-start.6
  5.8 23.2 %all-to-all-start = ((bf16[64,16,1024]{2,1,0:T(8,128)(2,1)}), bf16[64,16,1024]{2,1,0:T(8,128)(2,1)}, u32[]{:S(2)}, u32[]{:S(2)}) async-start(bf16[64,16,1024]{2,1,0:T(8,128)(2,1)} %bitcast.87), calls=%async_computation | async-start | bytes 4194304 | tf_op jit(solution)/shard_map/all_to_all | solution.py:43
  29.0 0.0 copy-done.5
  29.0 0.1 copy.25
  29.1 0.1 eq.53
  29.2 0.1 eq.57
  29.4 1.2 reduce-window.10
  30.6 0.2 slice_reduce_fusion
  30.8 0.1 fusion.19
  31.0 0.1 sub.40
  31.1 0.1 copy.28
  31.2 0.0 copy-done.7
  31.2 0.2 reduce-window.14
  31.4 0.7 fusion.30
  32.1 0.0 copy-done.4
  32.1 0.7 fusion.29
  32.7 0.1 convert_reduce_fusion
  32.8 0.0 copy-done.8
  32.8 9.9 %fusion.23 = s32[64]{0:T(128)S(1)} fusion(s32[64]{0:T(128)S(1)} %convert_reduce_fusion, s32[]{:T(128)} %bitcast.21, s32[]{:T(128)} %bitcast.10, s32[]{:T(128)} %bitcast.22, s32[]{:T(128)} %bitcast.11, s32[]{:T(128)} %bitcast.23, s32[]{:T(128)} %bitcast.12, s32[]{:T(128)} %bitcast.24, s32[]{:T(128)} %bitcast.13, s32[]{:T(128)} %bitcast.25, s32[]{:T(128)} %bitcast.14, ...), kind=kLoop, calls=%fused_computation.67 | loop fusion | flops 1792 | bytes 576 | tf_op jit(solution)/shard_map/add | solution.py:68
  42.8 0.1 select_reduce_fusion.1
  42.9 0.0 copy-done.6
  42.9 0.3 select_reduce_fusion
  43.2 2.0 %gather_fusion = f32[256,1024]{1,0:T(8,128)} fusion(f32[128,1024]{1,0:T(8,128)S(1)} %select_reduce_fusion, s32[1024]{0:T(1024)S(1)} %pad_clamp_fusion), kind=kCustom, calls=%fused_computation | custom fusion | bytes 2098176 | tf_op jit(solution)/shard_map/gather | solution.py:72
  45.2 1.4 select_convert_fusion
  46.7 0.0 copy-start.2
  46.7 0.8 copy-done.2
  47.5 0.0 copy-done.1
  47.5 1.0 subtract_convert_fusion
  48.5 75.4 %all-to-all-done = bf16[64,16,1024]{2,1,0:T(8,128)(2,1)} async-done(((bf16[64,16,1024]{2,1,0:T(8,128)(2,1)}), bf16[64,16,1024]{2,1,0:T(8,128)(2,1)}, u32[]{:S(2)}, u32[]{:S(2)}) %all-to-all-start) | async-done | bytes 2097184 | tf_op jit(solution)/shard_map/all_to_all | solution.py:43
  123.9 3.2 %fusion.1 = f32[512,1024]{1,0:T(8,128)S(1)} fusion(bf16[1024,1024]{1,0:T(8,128)(2,1)} %bitcast.2, bf16[256,1024]{1,0:T(8,128)(2,1)} %subtract_convert_fusion, bf16[256,1024]{1,0:T(8,128)(2,1)} %copy-done.2), kind=kOutput, calls=%fused_computation.11 | convolution fusion | flops 1075838976 | bytes 5242880 | tf_op jit(solution)/shard_map/dot_general | solution.py:78
  127.0 0.9 fusion
  128.0 13.3 %all-to-all-start.1 = ((bf16[16,16,1024]{2,1,0:T(8,128)(2,1)}), bf16[16,16,1024]{2,1,0:T(8,128)(2,1)}, u32[]{:S(2)}, u32[]{:S(2)}) async-start(bf16[16,16,1024]{2,1,0:T(8,128)(2,1)} %bitcast.86), calls=%async_computation.1 | async-start | bytes 1048576 | tf_op jit(solution)/shard_map/all_to_all | solution.py:83
  141.3 0.1 subtract_convert_fusion.1
  141.4 2.3 %fusion.14 = f32[256,1024]{1,0:T(8,128)S(1)} fusion(bf16[1024,1024]{1,0:T(8,128)(2,1)} %bitcast.2, bf16[128,1024]{1,0:T(8,128)(2,1)S(1)} %subtract_convert_fusion.1, bf16[128,1024]{1,0:T(8,128)(2,1)S(1)} %convert_element_type.51), kind=kOutput, calls=%fused_computation.28 | convolution fusion | flops 537919488 | bytes 3670016 | tf_op jit(solution)/shard_map/dot_general | solution.py:78
  143.7 0.8 fusion.13
  144.4 14.1 %all-to-all-done.1 = bf16[16,16,1024]{2,1,0:T(8,128)(2,1)} async-done(((bf16[16,16,1024]{2,1,0:T(8,128)(2,1)}), bf16[16,16,1024]{2,1,0:T(8,128)(2,1)}, u32[]{:S(2)}, u32[]{:S(2)}) %all-to-all-start.1) | async-done | bytes 524320 | tf_op jit(solution)/shard_map/all_to_all | solution.py:83
  158.6 0.0 copy-done
  158.6 1.9 %convolution_convert_fusion = bf16[256,1280]{1,0:T(8,128)(2,1)S(1)} fusion(bf16[256,1024]{1,0:T(8,128)(2,1)} %bitcast.31, bf16[1024,1280]{1,0:T(8,128)(2,1)S(1)} %copy-done), kind=kOutput, calls=%fused_computation.1 | convolution fusion | flops 671416320 | bytes 3801088 | tf_op jit(solution)/shard_map/dot_general | solution.py:88
  160.5 0.0 copy-start.3
  160.5 1.2 slice_convert_fusion
  161.7 2.4 %reshape.118 = f32[192,1280]{1,0:T(8,128)} reshape(f32[16,12,1280]{2,1,0:T(8,128)} %slice_convert_fusion) | data formatting | bytes 1966080 | tf_op jit(solution)/shard_map/convert_element_type | solution.py:94
  164.1 0.0 copy-done.3
  164.1 2.4 %fusion.12 = bf16[192,1280]{1,0:T(8,128)(2,1)} fusion(f32[192,1280]{1,0:T(8,128)} %reshape.118, bf16[192,1280]{1,0:T(8,128)(2,1)S(1)} %copy-done.3), kind=kLoop, calls=%fused_computation.24 | loop fusion | flops 2703360 | bytes 1966080 | tf_op jit(solution)/shard_map/convert_element_type | solution.py:94
  (14 shorter events, 0.1 us)
Async XLA Ops:
  0.6 158.0 %copy-start = (bf16[1024,1280]{1,0:T(8,128)(2,1)S(1)}, bf16[1024,1280]{1,0:T(8,128)(2,1)}, u32[]{:S(2)}) copy-start(bf16[1024,1280]{1,0:T(8,128)(2,1)} %param.13) | copy-start | bytes 7864324
  5.8 23.2 %copy-start.5 = (s32[128,4]{0,1:T(4,128)S(1)}, s32[128,4]{0,1:T(4,128)}, u32[]{:S(2)}) copy-start(s32[128,4]{0,1:T(4,128)} %param.9) | copy-start | bytes 6148
  5.8 25.4 %copy-start.7 = (s32[1,8]{1,0:T(1,128)S(1)}, s32[1,8]{1,0:T(1,128)}, u32[]{:S(2)}) copy-start(s32[1,8]{1,0:T(1,128)} %param.15) | copy-start | bytes 100
  5.8 26.3 %copy-start.4 = (s32[1,8]{1,0:T(1,128)S(1)}, s32[1,8]{1,0:T(1,128)}, u32[]{:S(2)}) copy-start(s32[1,8]{1,0:T(1,128)} %param.16) | copy-start | bytes 100
  5.8 27.0 %copy-start.8 = (s32[1,64]{1,0:T(1,128)S(1)}, s32[1,64]{1,0:T(1,128)}, u32[]{:S(2)}) copy-start(s32[1,64]{1,0:T(1,128)} %param.17) | copy-start | bytes 772
  5.8 37.1 %copy-start.6 = (f32[128,4]{0,1:T(4,128)S(1)}, f32[128,4]{0,1:T(4,128)}, u32[]{:S(2)}) copy-start(f32[128,4]{0,1:T(4,128)} %param.10) | copy-start | bytes 6148
  5.8 118.0 %all-to-all-start = ((bf16[64,16,1024]{2,1,0:T(8,128)(2,1)}), bf16[64,16,1024]{2,1,0:T(8,128)(2,1)}, u32[]{:S(2)}, u32[]{:S(2)}) async-start(bf16[64,16,1024]{2,1,0:T(8,128)(2,1)} %bitcast.87), calls=%async_computation | async-start | bytes 4194304 | tf_op jit(solution)/shard_map/all_to_all | solution.py:43
  45.2 2.3 %copy-start.1 = (f32[256,1024]{1,0:T(8,128)S(1)}, f32[256,1024]{1,0:T(8,128)}, u32[]{:S(2)}) copy-start(f32[256,1024]{1,0:T(8,128)} %gather_fusion) | copy-start | bytes 3145732
  46.7 0.8 copy-start.2
  128.0 30.6 %all-to-all-start.1 = ((bf16[16,16,1024]{2,1,0:T(8,128)(2,1)}), bf16[16,16,1024]{2,1,0:T(8,128)(2,1)}, u32[]{:S(2)}, u32[]{:S(2)}) async-start(bf16[16,16,1024]{2,1,0:T(8,128)(2,1)} %bitcast.86), calls=%async_computation.1 | async-start | bytes 1048576 | tf_op jit(solution)/shard_map/all_to_all | solution.py:83
  160.5 3.6 %copy-start.3 = (bf16[192,1280]{1,0:T(8,128)(2,1)S(1)}, bf16[192,1280]{1,0:T(8,128)(2,1)}, u32[]{:S(2)}) copy-start(bf16[192,1280]{1,0:T(8,128)(2,1)} %param.14) | copy-start | bytes 1474564

commit v5 on v3

--- a/solution.py
+++ b/solution.py
@@ -67,8 +67,7 @@
     place_at = owners[span_of] * span_cap + offset
     parcel_rows = jnp.arange(peer_count * span_cap, dtype=jnp.int32)
     lands = place_at[None, :] == parcel_rows[:, None]
-    token_of = jnp.sum(jnp.where(lands, positions[None, :] + 1, 0), axis=1) - 1
-    parcel_mix = jnp.where((token_of >= 0)[:, None], mix[jnp.maximum(token_of, 0)], 0.0)
+    audio_mix = mix[positions]
 
     def combine(weights_f32):
         hi = lax.optimization_barrier(weights_f32.astype(jnp.bfloat16))
@@ -77,7 +76,12 @@
         total = total + jnp.dot(lo, returned, preferred_element_type=jnp.float32)
         return total.astype(jnp.bfloat16)
 
-    parcel = combine(parcel_mix)
+    hi = lax.optimization_barrier(audio_mix.astype(jnp.bfloat16))
+    lo = (audio_mix - hi.astype(jnp.float32)).astype(jnp.bfloat16)
+    both = jnp.dot(jnp.concatenate([hi, lo]), returned, preferred_element_type=jnp.float32)
+    audio_rows = (both[:audio_count] + both[audio_count:]).astype(jnp.bfloat16)
+    parcel = jnp.dot(lands.astype(jnp.bfloat16), audio_rows, preferred_element_type=jnp.float32)
+    parcel = parcel.astype(jnp.bfloat16)
 
     arrived_rows = lax.all_to_all(
         parcel.reshape(peer_count, span_cap, D), "dp", split_axis=0, concat_axis=0, tiled=True

time: 166 us -> 162 us (0.976)
  matrix products: 15.8 us -> 13 us
  local copies, waits for them, and re-layouts: 7.29 us -> 5.15 us
  waiting for transfers between devices: 90.1 us -> 91.8 us
    dot_general x2 -> x1, matrix products: 5.72 us -> 2.74 us  [combine(): total = total + jnp.dot(lo, returned, preferred_element_type=jnp.float32)]
    dot_general x0 -> x2, matrix products: none -> 2.36 us  [the longest x1 2.11 us: body(): jnp.dot(jnp.concatenate([hi, lo]), returned, preferred_element_type=jnp.f...]
    dot_general x2 -> x1, matrix products: 4.27 us -> 2.03 us  [combine(): total = jnp.dot(hi, returned, preferred_element_type=jnp.float32)]
    all_to_all x1, waiting for transfers between devices: 77.6 us -> 79.3 us  [body(): lax.all_to_all(outgoing, 'expert', split_axis=0, concat_axis=0, tiled=True)]
where the time goes in v5:
time: 162 us; the launch traced here: 161 us
  waiting for transfers between devices  91.8 us (57%)
  starting transfers between devices  36.4 us (22%)
  other arithmetic  13.9 us (9%)
  matrix products  13 us (8%)
  local copies, waits for them, and re-layouts  5.15 us (3%)
    all_to_all x1, waiting for transfers between devices, body(): lax.all_to_all(outgoing, 'expert', split_axis=0, concat_axis=0, tiled=True)  79.3 us
    all_to_all x1, starting transfers between devices, body(): lax.all_to_all(outgoing, 'expert', split_axis=0, concat_axis=0, tiled=True)  23.2 us
    all_to_all x1, starting transfers between devices, body(): lax.all_to_all(parcel.reshape(peer_count, span_cap, D), 'dp', split_axis=...  13.3 us
    all_to_all x1, waiting for transfers between devices, body(): lax.all_to_all(parcel.reshape(peer_count, span_cap, D), 'dp', split_axis=...  12.5 us
    add x1, other arithmetic, body(): place_at = owners[span_of] * span_cap + offset  9.95 us
    dot_general x1, matrix products, body(): lax.dot_general(d_gate, gate_weight, (((1,), (1,)), ((), ())), preferred_...  5.15 us
  transfers between devices with their start and end apart: 2, of which 2 were waited for; matrix products, arithmetic and copies ran while one was open for 13% of the time, Pallas kernels for 0%

profile of v5, /device:TPU:1, one launch (start us, length us, event | category | flops | bytes accessed | tf_op | source)
XLA Modules:
  0.0 161.1 jit_solution(8862493593429598495)
XLA Ops:
  0.6 0.0 copy-start
  0.6 5.1 %convolution_convert_fusion.1 = bf16[1024,1024]{1,0:T(8,128)(2,1)} fusion(bf16[1024,768]{1,0:T(8,128)(2,1)} %param.11, bf16[1024,768]{1,0:T(8,128)(2,1)} %param.12), kind=kOutput, calls=%fused_computation.4 | convolution fusion | flops 1611661312 | bytes 5242880 | tf_op jit(solution)/shard_map/dot_general | solution.py:35
  5.8 0.0 copy-start.3
  5.8 0.0 copy-start.5
  5.8 0.0 copy-start.4
  5.8 23.2 %all-to-all-start = ((bf16[64,16,1024]{2,1,0:T(8,128)(2,1)}), bf16[64,16,1024]{2,1,0:T(8,128)(2,1)}, u32[]{:S(2)}, u32[]{:S(2)}) async-start(bf16[64,16,1024]{2,1,0:T(8,128)(2,1)} %bitcast.87), calls=%async_computation | async-start | bytes 4194304 | tf_op jit(solution)/shard_map/all_to_all | solution.py:43
  29.0 0.0 copy-done.3
  29.0 0.1 copy.25
  29.1 0.1 eq.53
  29.2 0.0 copy-start.6
  29.2 0.0 copy-start.2
  29.2 0.1 eq.57
  29.4 1.2 reduce-window.10
  30.6 0.2 slice_reduce_fusion
  30.8 0.1 fusion.16
  31.0 0.1 sub.36
  31.1 0.1 copy.28
  31.1 0.0 copy-done.5
  31.2 0.0 copy-done.4
  31.2 0.3 select_reduce_fusion
  31.5 0.7 gather_fusion
  32.2 0.0 copy-done.6
  32.2 0.2 reduce-window.14
  32.4 0.7 fusion.28
  33.1 0.0 copy-done.2
  33.1 0.7 fusion.27
  33.8 0.1 convert_reduce_fusion
  33.8 9.9 %fusion.21 = s32[64]{0:T(128)S(1)} fusion(s32[64]{0:T(128)S(1)} %convert_reduce_fusion, s32[]{:T(128)} %bitcast.21, s32[]{:T(128)} %bitcast.10, s32[]{:T(128)} %bitcast.22, s32[]{:T(128)} %bitcast.11, s32[]{:T(128)} %bitcast.23, s32[]{:T(128)} %bitcast.12, s32[]{:T(128)} %bitcast.24, s32[]{:T(128)} %bitcast.13, s32[]{:T(128)} %bitcast.25, s32[]{:T(128)} %bitcast.14, ...), kind=kLoop, calls=%fused_computation.61 | loop fusion | flops 1792 | bytes 576 | tf_op jit(solution)/shard_map/add | solution.py:67
  43.8 0.7 subtract_convert_fusion.2
  44.5 79.3 %all-to-all-done = bf16[64,16,1024]{2,1,0:T(8,128)(2,1)} async-done(((bf16[64,16,1024]{2,1,0:T(8,128)(2,1)}), bf16[64,16,1024]{2,1,0:T(8,128)(2,1)}, u32[]{:S(2)}, u32[]{:S(2)}) %all-to-all-start) | async-done | bytes 2097184 | tf_op jit(solution)/shard_map/all_to_all | solution.py:43
  123.8 2.1 %fusion.10 = f32[128,1024]{1,0:T(8,128)S(1)} fusion(bf16[1024,1024]{1,0:T(8,128)(2,1)} %bitcast.2, bf16[64,1024]{1,0:T(8,128)(2,1)} %subtract_convert_fusion.2, bf16[64,1024]{1,0:T(8,128)(2,1)S(1)} %convert_element_type.58), kind=kOutput, calls=%fused_computation.23 | convolution fusion | flops 268959744 | bytes 2883584 | tf_op jit(solution)/shard_map/dot_general | solution.py:81
  126.0 0.3 convolution_convert_fusion.2
  126.2 0.9 reshape.120
  127.1 13.3 %all-to-all-start.1 = ((bf16[16,12,1024]{2,1,0:T(8,128)(2,1)}), bf16[16,12,1024]{2,1,0:T(8,128)(2,1)}, u32[]{:S(2)}, u32[]{:S(2)}) async-start(bf16[16,12,1024]{2,1,0:T(8,128)(2,1)} %reshape.120), calls=%async_computation.1 | async-start | bytes 1048576 | tf_op jit(solution)/shard_map/all_to_all | solution.py:86
  140.4 2.0 %fusion.29 = f32[128,1024]{1,0:T(8,128)S(1)} fusion(bf16[128,1024]{1,0:T(8,128)(2,1)S(1)} %convert_element_type.52, bf16[1024,1024]{1,0:T(8,128)(2,1)} %bitcast.2), kind=kOutput, calls=%fused_computation.71 | convolution fusion | flops 268435456 | bytes 2883584 | tf_op jit(solution)/shard_map/dot_general | solution.py:75
  142.5 2.7 %fusion = bf16[128,1024]{1,0:T(8,128)(2,1)} fusion(f32[128,1024]{1,0:T(8,128)S(1)} %fusion.29, bf16[1024,1024]{1,0:T(8,128)(2,1)} %bitcast.2, f32[128,1024]{1,0:T(8,128)S(1)} %select_reduce_fusion, bf16[128,1024]{1,0:T(8,128)(2,1)S(1)} %convert_element_type.52), kind=kOutput, calls=%fused_computation.11 | convolution fusion | flops 269090816 | bytes 3670016 | tf_op jit(solution)/shard_map/dot_general | solution.py:76
  145.2 12.5 %all-to-all-done.1 = bf16[16,12,1024]{2,1,0:T(8,128)(2,1)} async-done(((bf16[16,12,1024]{2,1,0:T(8,128)(2,1)}), bf16[16,12,1024]{2,1,0:T(8,128)(2,1)}, u32[]{:S(2)}, u32[]{:S(2)}) %all-to-all-start.1) | async-done | bytes 393248 | tf_op jit(solution)/shard_map/all_to_all | solution.py:86
  157.7 1.1 reshape.121
  158.8 0.0 copy-done
  158.8 0.0 copy-start.1
  158.9 0.7 convolution_convert_fusion
  159.6 0.3 copy-done.1
  159.9 1.2 fusion.8
  (11 shorter events, 0.1 us)
Async XLA Ops:
  0.6 158.2 %copy-start = (bf16[1024,1280]{1,0:T(8,128)(2,1)S(1)}, bf16[1024,1280]{1,0:T(8,128)(2,1)}, u32[]{:S(2)}) copy-start(bf16[1024,1280]{1,0:T(8,128)(2,1)} %param.13) | copy-start | bytes 7864324
  5.8 23.2 %copy-start.3 = (s32[128,4]{0,1:T(4,128)S(1)}, s32[128,4]{0,1:T(4,128)}, u32[]{:S(2)}) copy-start(s32[128,4]{0,1:T(4,128)} %param.9) | copy-start | bytes 6148
  5.8 25.4 %copy-start.5 = (s32[1,64]{1,0:T(1,128)S(1)}, s32[1,64]{1,0:T(1,128)}, u32[]{:S(2)}) copy-start(s32[1,64]{1,0:T(1,128)} %param.17) | copy-start | bytes 772
  5.8 25.4 %copy-start.4 = (f32[128,4]{0,1:T(4,128)S(1)}, f32[128,4]{0,1:T(4,128)}, u32[]{:S(2)}) copy-start(f32[128,4]{0,1:T(4,128)} %param.10) | copy-start | bytes 6148
  5.8 118.0 %all-to-all-start = ((bf16[64,16,1024]{2,1,0:T(8,128)(2,1)}), bf16[64,16,1024]{2,1,0:T(8,128)(2,1)}, u32[]{:S(2)}, u32[]{:S(2)}) async-start(bf16[64,16,1024]{2,1,0:T(8,128)(2,1)} %bitcast.87), calls=%async_computation | async-start | bytes 4194304 | tf_op jit(solution)/shard_map/all_to_all | solution.py:43
  29.2 3.0 %copy-start.6 = (s32[1,8]{1,0:T(1,128)S(1)}, s32[1,8]{1,0:T(1,128)}, u32[]{:S(2)}) copy-start(s32[1,8]{1,0:T(1,128)} %param.15) | copy-start | bytes 100
  29.2 3.9 %copy-start.2 = (s32[1,8]{1,0:T(1,128)S(1)}, s32[1,8]{1,0:T(1,128)}, u32[]{:S(2)}) copy-start(s32[1,8]{1,0:T(1,128)} %param.16) | copy-start | bytes 100
  127.1 30.6 %all-to-all-start.1 = ((bf16[16,12,1024]{2,1,0:T(8,128)(2,1)}), bf16[16,12,1024]{2,1,0:T(8,128)(2,1)}, u32[]{:S(2)}, u32[]{:S(2)}) async-start(bf16[16,12,1024]{2,1,0:T(8,128)(2,1)} %reshape.120), calls=%async_computation.1 | async-start | bytes 1048576 | tf_op jit(solution)/shard_map/all_to_all | solution.py:86
  158.8 1.0 copy-start.1

commit v6 on v5

--- a/solution.py
+++ b/solution.py
@@ -1,6 +1,7 @@
 import jax
 import jax.numpy as jnp
 from jax import lax
+from jax.experimental import pallas as pl
 from jax.sharding import PartitionSpec as P
 
 D = 1024
@@ -10,6 +11,28 @@
     normal_cdf = 0.5 * (1.0 + jax.scipy.special.erf(values * 0.7071067811865476))
     density = jnp.exp(-0.5 * values * values) * 0.3989422804014327
     return normal_cdf + values * density
+
+
+def rows_times_weights_t(rows, weights, block=256):
+    count, width = rows.shape
+    outs = weights.shape[0]
+
+    def kernel(x_ref, w_ref, o_ref):
+        acc = lax.dot_general(
+            x_ref[...], w_ref[...], (((1,), (1,)), ((), ())), preferred_element_type=jnp.float32
+        )
+        o_ref[...] = acc.astype(o_ref.dtype)
+
+    return pl.pallas_call(
+        kernel,
+        grid=(count // block,),
+        in_specs=[
+            pl.BlockSpec((block, width), lambda i: (i, 0)),
+            pl.BlockSpec((outs, width), lambda i: (0, 0)),
+        ],
+        out_specs=pl.BlockSpec((block, outs), lambda i: (i, 0)),
+        out_shape=jax.ShapeDtypeStruct((count, outs), jnp.bfloat16),
+    )(rows, weights)
 
 
 def body(
@@ -31,10 +54,8 @@
     hidden_width = gate_weight.shape[1]
     incoming = d_gate.reshape(groups, exp_dev, capacity_each, hidden_width)
     weights = gate_weight.reshape(exp_dev, D, hidden_width)
-    if exp_dev == 1:
-        outgoing = lax.dot_general(
-            d_gate, gate_weight, (((1,), (1,)), ((), ())), preferred_element_type=jnp.float32
-        )
+    if exp_dev == 1 and d_gate.shape[0] % 256 == 0:
+        outgoing = rows_times_weights_t(d_gate, gate_weight)
     else:
         outgoing = jnp.einsum(
             "sjrf,jdf->sjrd", incoming, weights, preferred_element_type=jnp.float32

time: 162 us -> 162 us (level)
  Pallas kernels: 0 us -> 5.55 us
  matrix products: 13 us -> 7.83 us
    pallas_call x0 -> x1, Pallas kernels: none -> 5.55 us  [rows_times_weights_t(): pl.pallas_call(kernel, grid=(count // block,), in_specs=[pl.BlockSpec((bl...]
    dot_general x1 -> x0, matrix products: 5.15 us -> none  [body(): lax.dot_general(d_gate, gate_weight, (((1,), (1,)), ((), ())), preferred_...]
  transfers between devices with their start and end apart: 2 -> 2, of which waited for: 2 -> 2; matrix products, arithmetic and copies ran while one was open for 13% -> 12% of each run, Pallas kernels for 0% -> 0%
where the time goes in v6:
time: 162 us
  waiting for transfers between devices  91.8 us (57%)
  starting transfers between devices  36.5 us (23%)
  other arithmetic  13.9 us (9%)
  matrix products  7.83 us (5%)
  Pallas kernels  5.55 us (3%)
  local copies, waits for them, and re-layouts  5.15 us (3%)
    all_to_all x1, waiting for transfers between devices, body(): lax.all_to_all(outgoing, 'expert', split_axis=0, concat_axis=0, tiled=True)  79.3 us
    all_to_all x1, starting transfers between devices, body(): lax.all_to_all(outgoing, 'expert', split_axis=0, concat_axis=0, tiled=True)  23.2 us
    all_to_all x1, starting transfers between devices, body(): lax.all_to_all(parcel.reshape(peer_count, span_cap, D), 'dp', split_axis=...  13.4 us
    all_to_all x1, waiting for transfers between devices, body(): lax.all_to_all(parcel.reshape(peer_count, span_cap, D), 'dp', split_axis=...  12.5 us
    add x1, other arithmetic, body(): place_at = owners[span_of] * span_cap + offset  9.95 us
    pallas_call x1, Pallas kernels, rows_times_weights_t(): pl.pallas_call(kernel, grid=(count // block,), in_specs=[pl.BlockSpec((bl...  5.55 us
  transfers between devices with their start and end apart: 2, of which 2 were waited for; matrix products, arithmetic and copies ran while one was open for 12% of the time, Pallas kernels for 0%

profile of v6, /device:TPU:1, one launch (start us, length us, event | category | flops | bytes accessed | tf_op | source)
XLA Modules:
  0.0 161.5 jit_solution(11427456917666659955)
XLA Ops:
  0.6 0.0 copy-start
  0.6 5.6 %shard_map.104 = bf16[1024,1024]{1,0:T(8,128)(2,1)} custom-call(bf16[1024,768]{1,0:T(8,128)(2,1)} %x_ref.1, bf16[1024,768]{1,0:T(8,128)(2,1)} %w_ref.1), custom_call_target="tpu_custom_call" | custom-call | tf_op jit(solution)/shard_map/pallas_call | solution.py:26
  6.2 0.0 copy-start.3
  6.2 0.0 copy-start.5
  6.2 0.0 copy-start.4
  6.2 23.2 %all-to-all-start = ((bf16[64,16,1024]{2,1,0:T(8,128)(2,1)}), bf16[64,16,1024]{2,1,0:T(8,128)(2,1)}, u32[]{:S(2)}, u32[]{:S(2)}) async-start(bf16[64,16,1024]{2,1,0:T(8,128)(2,1)} %bitcast.85), calls=%async_computation | async-start | bytes 4194304 | tf_op jit(solution)/shard_map/all_to_all | solution.py:64
  29.4 0.0 copy-done.3
  29.4 0.1 copy.25
  29.5 0.1 eq.53
  29.6 0.0 copy-start.6
  29.6 0.0 copy-start.2
  29.6 0.1 eq.57
  29.8 1.2 reduce-window.10
  31.0 0.2 slice_reduce_fusion
  31.3 0.1 fusion.16
  31.4 0.1 sub.36
  31.5 0.1 copy.28
  31.6 0.0 copy-done.5
  31.6 0.0 copy-done.4
  31.6 0.3 select_reduce_fusion
  31.9 0.7 gather_fusion
  32.6 0.0 copy-done.6
  32.6 0.2 reduce-window.14
  32.8 0.7 fusion.28
  33.5 0.0 copy-done.2
  33.5 0.7 fusion.27
  34.2 0.1 convert_reduce_fusion
  34.3 9.9 %fusion.21 = s32[64]{0:T(128)S(1)} fusion(s32[64]{0:T(128)S(1)} %convert_reduce_fusion, s32[]{:T(128)} %bitcast.21, s32[]{:T(128)} %bitcast.10, s32[]{:T(128)} %bitcast.22, s32[]{:T(128)} %bitcast.11, s32[]{:T(128)} %bitcast.23, s32[]{:T(128)} %bitcast.12, s32[]{:T(128)} %bitcast.24, s32[]{:T(128)} %bitcast.13, s32[]{:T(128)} %bitcast.25, s32[]{:T(128)} %bitcast.14, ...), kind=kLoop, calls=%fused_computation.60 | loop fusion | flops 1792 | bytes 576 | tf_op jit(solution)/shard_map/add | solution.py:88
  44.2 0.7 subtract_convert_fusion.2
  44.9 79.3 %all-to-all-done = bf16[64,16,1024]{2,1,0:T(8,128)(2,1)} async-done(((bf16[64,16,1024]{2,1,0:T(8,128)(2,1)}), bf16[64,16,1024]{2,1,0:T(8,128)(2,1)}, u32[]{:S(2)}, u32[]{:S(2)}) %all-to-all-start) | async-done | bytes 2097184 | tf_op jit(solution)/shard_map/all_to_all | solution.py:64
  124.2 2.1 %fusion.10 = f32[128,1024]{1,0:T(8,128)S(1)} fusion(bf16[1024,1024]{1,0:T(8,128)(2,1)} %bitcast.2, bf16[64,1024]{1,0:T(8,128)(2,1)} %subtract_convert_fusion.2, bf16[64,1024]{1,0:T(8,128)(2,1)S(1)} %convert_element_type.54), kind=kOutput, calls=%fused_computation.22 | convolution fusion | flops 268959744 | bytes 2883584 | tf_op jit(solution)/shard_map/dot_general | solution.py:102
  126.3 0.3 convolution_convert_fusion.1
  126.6 0.9 reshape.120
  127.5 13.4 %all-to-all-start.1 = ((bf16[16,12,1024]{2,1,0:T(8,128)(2,1)}), bf16[16,12,1024]{2,1,0:T(8,128)(2,1)}, u32[]{:S(2)}, u32[]{:S(2)}) async-start(bf16[16,12,1024]{2,1,0:T(8,128)(2,1)} %reshape.120), calls=%async_computation.1 | async-start | bytes 1048576 | tf_op jit(solution)/shard_map/all_to_all | solution.py:107
  140.9 2.0 %fusion.29 = f32[128,1024]{1,0:T(8,128)S(1)} fusion(bf16[128,1024]{1,0:T(8,128)(2,1)S(1)} %convert_element_type.49, bf16[1024,1024]{1,0:T(8,128)(2,1)} %bitcast.2), kind=kOutput, calls=%fused_computation.70 | convolution fusion | flops 268435456 | bytes 2883584 | tf_op jit(solution)/shard_map/dot_general | solution.py:96
  142.9 2.7 %fusion = bf16[128,1024]{1,0:T(8,128)(2,1)} fusion(f32[128,1024]{1,0:T(8,128)S(1)} %fusion.29, bf16[1024,1024]{1,0:T(8,128)(2,1)} %bitcast.2, f32[128,1024]{1,0:T(8,128)S(1)} %select_reduce_fusion, bf16[128,1024]{1,0:T(8,128)(2,1)S(1)} %convert_element_type.49), kind=kOutput, calls=%fused_computation.10 | convolution fusion | flops 269090816 | bytes 3670016 | tf_op jit(solution)/shard_map/dot_general | solution.py:97
  145.6 12.5 %all-to-all-done.1 = bf16[16,12,1024]{2,1,0:T(8,128)(2,1)} async-done(((bf16[16,12,1024]{2,1,0:T(8,128)(2,1)}), bf16[16,12,1024]{2,1,0:T(8,128)(2,1)}, u32[]{:S(2)}, u32[]{:S(2)}) %all-to-all-start.1) | async-done | bytes 393248 | tf_op jit(solution)/shard_map/all_to_all | solution.py:107
  158.1 1.1 reshape.121
  159.3 0.0 copy-done
  159.3 0.0 copy-start.1
  159.3 0.7 convolution_convert_fusion
  160.0 0.3 copy-done.1
  160.3 1.2 fusion.8
  (11 shorter events, 0.1 us)
Async XLA Ops:
  0.6 158.6 %copy-start = (bf16[1024,1280]{1,0:T(8,128)(2,1)S(1)}, bf16[1024,1280]{1,0:T(8,128)(2,1)}, u32[]{:S(2)}) copy-start(bf16[1024,1280]{1,0:T(8,128)(2,1)} %param.13) | copy-start | bytes 7864324
  6.2 23.2 %copy-start.3 = (s32[128,4]{0,1:T(4,128)S(1)}, s32[128,4]{0,1:T(4,128)}, u32[]{:S(2)}) copy-start(s32[128,4]{0,1:T(4,128)} %param.9) | copy-start | bytes 6148
  6.2 25.4 %copy-start.5 = (s32[1,64]{1,0:T(1,128)S(1)}, s32[1,64]{1,0:T(1,128)}, u32[]{:S(2)}) copy-start(s32[1,64]{1,0:T(1,128)} %param.17) | copy-start | bytes 772
  6.2 25.4 %copy-start.4 = (f32[128,4]{0,1:T(4,128)S(1)}, f32[128,4]{0,1:T(4,128)}, u32[]{:S(2)}) copy-start(f32[128,4]{0,1:T(4,128)} %param.10) | copy-start | bytes 6148
  6.2 118.0 %all-to-all-start = ((bf16[64,16,1024]{2,1,0:T(8,128)(2,1)}), bf16[64,16,1024]{2,1,0:T(8,128)(2,1)}, u32[]{:S(2)}, u32[]{:S(2)}) async-start(bf16[64,16,1024]{2,1,0:T(8,128)(2,1)} %bitcast.85), calls=%async_computation | async-start | bytes 4194304 | tf_op jit(solution)/shard_map/all_to_all | solution.py:64
  29.6 3.0 %copy-start.6 = (s32[1,8]{1,0:T(1,128)S(1)}, s32[1,8]{1,0:T(1,128)}, u32[]{:S(2)}) copy-start(s32[1,8]{1,0:T(1,128)} %param.15) | copy-start | bytes 100
  29.6 3.9 %copy-start.2 = (s32[1,8]{1,0:T(1,128)S(1)}, s32[1,8]{1,0:T(1,128)}, u32[]{:S(2)}) copy-start(s32[1,8]{1,0:T(1,128)} %param.16) | copy-start | bytes 100
  127.5 30.7 %all-to-all-start.1 = ((bf16[16,12,1024]{2,1,0:T(8,128)(2,1)}), bf16[16,12,1024]{2,1,0:T(8,128)(2,1)}, u32[]{:S(2)}, u32[]{:S(2)}) async-start(bf16[16,12,1024]{2,1,0:T(8,128)(2,1)} %reshape.120), calls=%async_computation.1 | async-start | bytes 1048576 | tf_op jit(solution)/shard_map/all_to_all | solution.py:107
  159.3 1.0 copy-start.1

commit v7 on v5

--- a/solution.py
+++ b/solution.py
@@ -1,6 +1,7 @@
 import jax
 import jax.numpy as jnp
 from jax import lax
+from jax.experimental import pallas as pl
 from jax.sharding import PartitionSpec as P
 
 D = 1024
@@ -10,6 +11,23 @@
     normal_cdf = 0.5 * (1.0 + jax.scipy.special.erf(values * 0.7071067811865476))
     density = jnp.exp(-0.5 * values * values) * 0.3989422804014327
     return normal_cdf + values * density
+
+
+def audio_parcel(stacked, returned, lands):
+    count = stacked.shape[0] // 2
+    owners, cap, _ = lands.shape
+
+    def kernel(s_ref, r_ref, l_ref, o_ref):
+        both = jnp.dot(s_ref[...], r_ref[...], preferred_element_type=jnp.float32)
+        rows = (both[:count] + both[count:]).astype(jnp.bfloat16)
+        for owner in range(owners):
+            placed = jnp.dot(l_ref[owner], rows, preferred_element_type=jnp.float32)
+            o_ref[owner] = placed.astype(o_ref.dtype)
+
+    return pl.pallas_call(
+        kernel,
+        out_shape=jax.ShapeDtypeStruct((owners, cap, returned.shape[1]), jnp.bfloat16),
+    )(stacked, returned, lands)
 
 
 def body(
@@ -78,14 +96,10 @@
 
     hi = lax.optimization_barrier(audio_mix.astype(jnp.bfloat16))
     lo = (audio_mix - hi.astype(jnp.float32)).astype(jnp.bfloat16)
-    both = jnp.dot(jnp.concatenate([hi, lo]), returned, preferred_element_type=jnp.float32)
-    audio_rows = (both[:audio_count] + both[audio_count:]).astype(jnp.bfloat16)
-    parcel = jnp.dot(lands.astype(jnp.bfloat16), audio_rows, preferred_element_type=jnp.float32)
-    parcel = parcel.astype(jnp.bfloat16)
+    lands = lands.astype(jnp.bfloat16).reshape(peer_count, span_cap, audio_count)
+    parcel = audio_parcel(jnp.concatenate([hi, lo]), returned, lands)
 
-    arrived_rows = lax.all_to_all(
-        parcel.reshape(peer_count, span_cap, D), "dp", split_axis=0, concat_axis=0, tiled=True
-    )
+    arrived_rows = lax.all_to_all(parcel, "dp", split_axis=0, concat_axis=0, tiled=True)
     arrived_rows = arrived_rows.reshape(peer_count * span_cap, D)
     token_grad = combine(mix)
     arrived = jnp.dot(arrived_rows, projector, preferred_element_type=jnp.float32).astype(

time: 162 us -> 162 us (level)
  Pallas kernels: 0 us -> 3.24 us
  matrix products: 13 us -> 10.6 us
    pallas_call x0 -> x1, Pallas kernels: none -> 3.24 us  [audio_parcel(): pl.pallas_call(kernel, out_shape=jax.ShapeDtypeStruct((owners, cap, retur...]
    dot_general x2 -> x0, matrix products: 2.36 us -> none  [the longest x1 2.11 us: body(): jnp.dot(jnp.concatenate([hi, lo]), returned, preferred_element_type=jnp.f...]
where the time goes in v7:
time: 162 us; the launch traced here: 161 us
  waiting for transfers between devices  91 us (56%)
  starting transfers between devices  36.4 us (22%)
  other arithmetic  14.7 us (9%)
  matrix products  10.6 us (7%)
  local copies, waits for them, and re-layouts  4.27 us (3%)
  Pallas kernels  3.24 us (2%)
    all_to_all x1, waiting for transfers between devices, body(): lax.all_to_all(outgoing, 'expert', split_axis=0, concat_axis=0, tiled=True)  78.5 us
    all_to_all x1, starting transfers between devices, body(): lax.all_to_all(outgoing, 'expert', split_axis=0, concat_axis=0, tiled=True)  23.2 us
    all_to_all x1, starting transfers between devices, body(): lax.all_to_all(parcel, 'dp', split_axis=0, concat_axis=0, tiled=True)  13.3 us
    all_to_all x1, waiting for transfers between devices, body(): lax.all_to_all(parcel, 'dp', split_axis=0, concat_axis=0, tiled=True)  12.5 us
    add x1, other arithmetic, body(): place_at = owners[span_of] * span_cap + offset  9.98 us
    dot_general x1, matrix products, body(): lax.dot_general(d_gate, gate_weight, (((1,), (1,)), ((), ())), preferred_...  5.15 us
  transfers between devices with their start and end apart: 2, of which 2 were waited for; matrix products, arithmetic and copies ran while one was open for 13% of the time, Pallas kernels for 0%

profile of v7, /device:TPU:1, one launch (start us, length us, event | category | flops | bytes accessed | tf_op | source)
XLA Modules:
  0.0 161.1 jit_solution(14616089831039581466)
XLA Ops:
  0.6 0.0 copy-start
  0.6 5.1 %convolution_convert_fusion.1 = bf16[1024,1024]{1,0:T(8,128)(2,1)} fusion(bf16[1024,768]{1,0:T(8,128)(2,1)} %param.11, bf16[1024,768]{1,0:T(8,128)(2,1)} %param.12), kind=kOutput, calls=%fused_computation.4 | convolution fusion | flops 1611661312 | bytes 5242880 | tf_op jit(solution)/shard_map/dot_general | solution.py:53
  5.8 0.0 copy-start.3
  5.8 0.0 copy-start.5
  5.8 0.0 copy-start.4
  5.8 23.2 %all-to-all-start = ((bf16[64,16,1024]{2,1,0:T(8,128)(2,1)}), bf16[64,16,1024]{2,1,0:T(8,128)(2,1)}, u32[]{:S(2)}, u32[]{:S(2)}) async-start(bf16[64,16,1024]{2,1,0:T(8,128)(2,1)} %bitcast.86), calls=%async_computation | async-start | bytes 4194304 | tf_op jit(solution)/shard_map/all_to_all | solution.py:61
  29.0 0.0 copy-done.3
  29.0 0.1 copy.25
  29.1 0.1 eq.60
  29.2 0.0 copy-start.6
  29.2 0.0 copy-start.2
  29.2 0.1 eq.64
  29.4 1.2 reduce-window.10
  30.6 0.2 slice_reduce_fusion
  30.8 0.1 fusion.10
  31.0 0.1 sub.36
  31.1 0.1 copy.28
  31.1 0.0 copy-done.5
  31.2 0.0 copy-done.4
  31.2 0.3 select_reduce_fusion
  31.5 0.7 gather_fusion
  32.2 0.0 copy-done.6
  32.2 0.2 reduce-window.14
  32.4 0.7 fusion.20
  33.1 0.0 copy-done.2
  33.1 0.7 fusion.19
  33.8 0.1 convert_reduce_fusion
  33.9 0.7 pad_maximum_fusion.s_ref
  34.6 10.0 %fusion.14 = s32[64]{0:T(128)S(1)} fusion(s32[64]{0:T(128)S(1)} %convert_reduce_fusion, s32[]{:T(128)} %bitcast.23, s32[]{:T(128)} %bitcast.12, s32[]{:T(128)} %bitcast.24, s32[]{:T(128)} %bitcast.13, s32[]{:T(128)} %bitcast.25, s32[]{:T(128)} %bitcast.14, s32[]{:T(128)} %bitcast.26, s32[]{:T(128)} %bitcast.15, s32[]{:T(128)} %bitcast.27, s32[]{:T(128)} %bitcast.16, ...), kind=kLoop, calls=%fused_computation.55 | loop fusion | flops 1792 | bytes 576 | tf_op jit(solution)/shard_map/add | solution.py:85
  44.6 0.7 compare_convert_fusion.l_ref
  45.3 78.5 %all-to-all-done = bf16[64,16,1024]{2,1,0:T(8,128)(2,1)} async-done(((bf16[64,16,1024]{2,1,0:T(8,128)(2,1)}), bf16[64,16,1024]{2,1,0:T(8,128)(2,1)}, u32[]{:S(2)}, u32[]{:S(2)}) %all-to-all-start) | async-done | bytes 2097184 | tf_op jit(solution)/shard_map/all_to_all | solution.py:61
  123.8 3.2 %shard_map.104 = bf16[16,12,1024]{2,1,0:T(8,128)(2,1)} custom-call(bf16[128,1024]{1,0:T(8,128)(2,1)} %pad_maximum_fusion.s_ref, bf16[1024,1024]{1,0:T(8,128)(2,1)} %bitcast.2.r_ref, bf16[16,12,64]{2,1,0:T(8,128)(2,1)} %compare_convert_fusion.l_ref), custom_call_target="tpu_custom_call" | custom-call | tf_op jit(solution)/shard_map/pallas_call | solution.py:27
  127.1 13.3 %all-to-all-start.1 = ((bf16[16,12,1024]{2,1,0:T(8,128)(2,1)}), bf16[16,12,1024]{2,1,0:T(8,128)(2,1)}, u32[]{:S(2)}, u32[]{:S(2)}) async-start(bf16[16,12,1024]{2,1,0:T(8,128)(2,1)} %shard_map.104), calls=%async_computation.1 | async-start | bytes 1048576 | tf_op jit(solution)/shard_map/all_to_all | solution.py:102
  140.4 2.0 %fusion.21 = f32[128,1024]{1,0:T(8,128)S(1)} fusion(bf16[128,1024]{1,0:T(8,128)(2,1)S(1)} %convert_element_type.49, bf16[1024,1024]{1,0:T(8,128)(2,1)} %bitcast.2.r_ref), kind=kOutput, calls=%fused_computation.64 | convolution fusion | flops 268435456 | bytes 2883584 | tf_op jit(solution)/shard_map/dot_general | solution.py:93
  142.4 2.7 %fusion = bf16[128,1024]{1,0:T(8,128)(2,1)} fusion(f32[128,1024]{1,0:T(8,128)S(1)} %fusion.21, bf16[1024,1024]{1,0:T(8,128)(2,1)} %bitcast.2.r_ref, f32[128,1024]{1,0:T(8,128)S(1)} %select_reduce_fusion, bf16[128,1024]{1,0:T(8,128)(2,1)S(1)} %convert_element_type.49), kind=kOutput, calls=%fused_computation.10 | convolution fusion | flops 269090816 | bytes 3670016 | tf_op jit(solution)/shard_map/dot_general | solution.py:94
  145.2 12.5 %all-to-all-done.1 = bf16[16,12,1024]{2,1,0:T(8,128)(2,1)} async-done(((bf16[16,12,1024]{2,1,0:T(8,128)(2,1)}), bf16[16,12,1024]{2,1,0:T(8,128)(2,1)}, u32[]{:S(2)}, u32[]{:S(2)}) %all-to-all-start.1) | async-done | bytes 393248 | tf_op jit(solution)/shard_map/all_to_all | solution.py:102
  157.7 1.1 reshape.132
  158.8 0.0 copy-done
  158.8 0.0 copy-start.1
  158.8 0.7 convolution_convert_fusion
  159.5 0.3 copy-done.1
  159.8 1.2 fusion.8
  (13 shorter events, 0.2 us)
Async XLA Ops:
  0.6 158.2 %copy-start = (bf16[1024,1280]{1,0:T(8,128)(2,1)S(1)}, bf16[1024,1280]{1,0:T(8,128)(2,1)}, u32[]{:S(2)}) copy-start(bf16[1024,1280]{1,0:T(8,128)(2,1)} %param.13) | copy-start | bytes 7864324
  5.8 23.2 %copy-start.3 = (s32[128,4]{0,1:T(4,128)S(1)}, s32[128,4]{0,1:T(4,128)}, u32[]{:S(2)}) copy-start(s32[128,4]{0,1:T(4,128)} %param.9) | copy-start | bytes 6148
  5.8 25.4 %copy-start.5 = (s32[1,64]{1,0:T(1,128)S(1)}, s32[1,64]{1,0:T(1,128)}, u32[]{:S(2)}) copy-start(s32[1,64]{1,0:T(1,128)} %param.17) | copy-start | bytes 772
  5.8 25.4 %copy-start.4 = (f32[128,4]{0,1:T(4,128)S(1)}, f32[128,4]{0,1:T(4,128)}, u32[]{:S(2)}) copy-start(f32[128,4]{0,1:T(4,128)} %param.10) | copy-start | bytes 6148
  5.8 118.0 %all-to-all-start = ((bf16[64,16,1024]{2,1,0:T(8,128)(2,1)}), bf16[64,16,1024]{2,1,0:T(8,128)(2,1)}, u32[]{:S(2)}, u32[]{:S(2)}) async-start(bf16[64,16,1024]{2,1,0:T(8,128)(2,1)} %bitcast.86), calls=%async_computation | async-start | bytes 4194304 | tf_op jit(solution)/shard_map/all_to_all | solution.py:61
  29.2 3.0 %copy-start.6 = (s32[1,8]{1,0:T(1,128)S(1)}, s32[1,8]{1,0:T(1,128)}, u32[]{:S(2)}) copy-start(s32[1,8]{1,0:T(1,128)} %param.15) | copy-start | bytes 100
  29.2 3.9 %copy-start.2 = (s32[1,8]{1,0:T(1,128)S(1)}, s32[1,8]{1,0:T(1,128)}, u32[]{:S(2)}) copy-start(s32[1,8]{1,0:T(1,128)} %param.16) | copy-start | bytes 100
  127.1 30.6 %all-to-all-start.1 = ((bf16[16,12,1024]{2,1,0:T(8,128)(2,1)}), bf16[16,12,1024]{2,1,0:T(8,128)(2,1)}, u32[]{:S(2)}, u32[]{:S(2)}) async-start(bf16[16,12,1024]{2,1,0:T(8,128)(2,1)} %shard_map.104), calls=%async_computation.1 | async-start | bytes 1048576 | tf_op jit(solution)/shard_map/all_to_all | solution.py:102
  158.8 1.0 copy-start.1
